TPU v7x, 512 devices: a whole 4x4x16 slice. The times are simulated.
512 devices in a mesh: site: 32 (over z_hi, y, core), shard: 16 (over x, z_lo).
Axes of the slice: x: 4, y: 4, z: 16 (z_hi: 4, z_lo: 4; z = z_hi * 4 + z_lo), core: 2. Of those that a mesh axis runs over, the one named last changes fastest.
Arguments:
- activations: bfloat16 [65536, 2560], P(('site', 'shard')), may hold values from -6 to 6
- out_grads: bfloat16 [65536, 5120], P(('site', 'shard')), may hold values from -6 to 6
- theta: bfloat16 [32, 2560, 5120], P('site', None, 'shard'), may hold values from -6 to 6
- token_ids: int32 [65536], P(('site', 'shard')), may hold values from 0 to 31999
- assignment: int32 [32, 2048], P('site'), may hold values from 0 to 2047, each once within a row
Outputs:
- merged: bfloat16 [2560, 5120], P('site', 'shard')
- response: bfloat16 [16384, 5120], P('site', 'shard')
Inputs may be any that keep to these rules, and one draw needn't show every extreme that they name: Each row of assignment holds every site position 0 to 2047 once.
All inputs are finite; a program needn't handle non-finite values.
Results may differ from a plain program's by a relative error of at most 0.02.
Values may be sent and summed in bfloat16 or wider, within the bound.
No kernel may reach another device: no remote copies, remote signals or barrier semaphores. Data moves between devices by JAX's collectives and lax.ppermute only.
A program may use at most 64 MiB of HBM per device.

v0:
```python
import math

import jax
import jax.numpy as jnp
from jax import lax
from jax.sharding import PartitionSpec as P

HEADS = 20
HEAD_DIM = 128
MICRO = 4


epsilon = 1e-06


def count_same(site_ids):
    site_events = site_ids.shape[0]
    block_rows = math.gcd(site_events, 512)
    blocks = site_ids.reshape(site_events // block_rows, block_rows)

    def one_block(block_ids):
        return jnp.sum((block_ids[:, None] == site_ids[None, :]).astype(jnp.int32), axis=1)

    return lax.map(one_block, blocks).reshape(site_events)


def on_device(activations, out_grads, theta, token_ids, assignment):
    head_cols = HEADS * HEAD_DIM
    site_ids = lax.all_gather(token_ids, "shard", axis=0, tiled=True)
    site_acts = lax.all_gather(activations, "shard", axis=0, tiled=True)
    grad_cols = lax.all_to_all(out_grads, "shard", split_axis=1, concat_axis=0, tiled=True)
    site_events = site_acts.shape[0]
    micro_rows = site_events // MICRO
    ordering = assignment[0]
    counts = count_same(site_ids)
    weights = 1.0 / counts.astype(jnp.float32)
    fisher = jnp.zeros((head_cols, grad_cols.shape[1]), jnp.float32)
    for micro in range(MICRO):
        picked = ordering[micro * micro_rows : (micro + 1) * micro_rows]
        acts_micro = jnp.take(site_acts, picked, axis=0)
        scaled = (
            jnp.take(grad_cols, picked, axis=0).astype(jnp.float32)
            * jnp.take(weights, picked)[:, None]
        ).astype(jnp.bfloat16)
        gradient = lax.dot_general(
            acts_micro, scaled, (((0,), (0,)), ((), ())), preferred_element_type=jnp.float32
        )
        fisher = fisher + gradient * gradient
    fisher = fisher / MICRO
    product = fisher * theta[0].astype(jnp.float32)
    numerator, denominator = (
        lax.psum_scatter(
            product.astype(jnp.bfloat16), "site", scatter_dimension=0, tiled=True
        ).astype(jnp.float32),
        lax.psum_scatter(
            fisher.astype(jnp.bfloat16), "site", scatter_dimension=0, tiled=True
        ).astype(jnp.float32),
    )
    owned = (numerator / (denominator + epsilon)).astype(jnp.bfloat16)
    whole_merged = lax.all_gather(owned, "site", axis=0, tiled=True)
    scaling = float(head_cols) ** (-0.5)
    probe = jnp.take(site_acts, ordering[:micro_rows], axis=0)
    response = (jnp.dot(probe, whole_merged, preferred_element_type=jnp.float32) * scaling).astype(
        jnp.bfloat16
    )
    return (owned, response)


def solution(mesh):
    placed = (
        P(("site", "shard"), None),
        P(("site", "shard"), None),
        P("site", None, "shard"),
        P(("site", "shard")),
        P("site", None),
    )
    return jax.shard_map(
        on_device,
        mesh=mesh,
        in_specs=placed,
        out_specs=(P("site", "shard"), P("site", "shard")),
        check_vma=False,
    )
```

profile of v0, /device:TPU:1, one launch (start us, length us, event | category | flops | bytes accessed | tf_op | source)
XLA Modules:
  0.0 655.2 jit_solution(13683668272257869694)
XLA Ops:
  7.2 0.0 all-gather.4.cloned.1.call-start
  7.2 0.7 all-gather.4.cloned.1.call-update
  7.9 0.0 copy-start.3
  7.9 0.0 copy-start.2
  7.9 2.4 copy.16
  10.3 9.0 %all-to-all-start = ((bf16[128,16,320]{0,2,1:T(8,128)(2,1)}), bf16[128,16,320]{0,2,1:T(8,128)(2,1)S(1)}, u32[]{:S(2)}, u32[]{:S(2)}) async-start(bf16[128,16,320]{0,2,1:T(8,128)(2,1)} %bitcast.3), calls=%async_computation | async-start | bytes 2621440 | tf_op jit(solution)/shard_map/all_to_all | solution.py:31
  19.4 0.0 reduce-scatter.7.cloned.1.call-start
  19.4 80.2 %all-gather = s32[16,1,128]{2,1,0:T(1,128)S(1)} all-gather(s32[1,1,128]{2,1,0:T(1,128)S(1)} %bitcast.44), channel_id=1, replica_groups=mesh['site'=32,'shard'=16] {'shard'}, dimensions={0}, use_global_device_ids=true | all-gather | bytes 8704 | tf_op jit(solution)/shard_map/all_gather | solution.py:29
  99.6 0.5 broadcast.51
  100.1 0.7 reduce.3
  100.8 2.7 while.10
  100.8 0.6 convert_reduce_fusion.2
  101.5 0.6 convert_reduce_fusion.2
  102.2 0.6 convert_reduce_fusion.2
  102.9 0.6 convert_reduce_fusion.2
  103.6 3.1 gather_fusion.5
  106.8 3.1 gather_fusion.2
  109.9 3.1 gather_fusion.8
  113.1 3.1 gather_fusion.11
  116.3 0.0 all-to-all-done
  116.3 0.8 copy.17
  117.2 1.9 gather_fusion.4
  119.1 2.6 gather_fusion.1
  121.7 2.6 gather_fusion.7
  124.3 2.6 gather_fusion.10
  126.8 132.8 %all-gather.4.cloned.1.call-done = bf16[2048,2560]{1,0:T(8,128)(2,1)} async-done(((bf16[128,2560]{1,0:T(8,128)(2,1)}), bf16[2048,2560]{1,0:T(8,128)(2,1)}) %all-gather.4.cloned.1.call-update) | async-done | bytes 10485776 | tf_op jit(solution)/shard_map/all_gather | solution.py:30
  259.7 10.5 %gather_fusion.3 = bf16[512,2560]{1,0:T(8,128)(2,1)S(1)} fusion(bf16[2048,2560]{1,0:T(8,128)(2,1)} %all-gather.4.cloned.1.call-done, s32[1024]{0:T(1024)S(1)} %pad_clamp_fusion.2), kind=kCustom, calls=%fused_computation.3.clone | custom fusion | bytes 5244928 | tf_op jit(solution)/shard_map/jit(_take)/gather | solution.py:40
  270.2 3.0 convolution_multiply_fusion.2
  273.3 11.6 %gather_fusion = bf16[512,2560]{1,0:T(8,128)(2,1)} fusion(bf16[2048,2560]{1,0:T(8,128)(2,1)} %all-gather.4.cloned.1.call-done, s32[1024]{0:T(1024)S(1)} %pad_clamp_fusion.3), kind=kCustom, calls=%fused_computation.clone | custom fusion | bytes 5244928 | tf_op jit(solution)/shard_map/jit(_take)/gather | solution.py:40
  284.9 4.1 fusion
  288.9 11.4 %gather_fusion.6 = bf16[512,2560]{1,0:T(8,128)(2,1)} fusion(bf16[2048,2560]{1,0:T(8,128)(2,1)} %all-gather.4.cloned.1.call-done, s32[1024]{0:T(1024)S(1)} %pad_clamp_fusion.1), kind=kCustom, calls=%fused_computation.4.clone | custom fusion | bytes 5244928 | tf_op jit(solution)/shard_map/jit(_take)/gather | solution.py:40
  300.4 4.8 fusion.1
  305.2 11.8 %gather_fusion.9 = bf16[512,2560]{1,0:T(8,128)(2,1)} fusion(bf16[2048,2560]{1,0:T(8,128)(2,1)} %all-gather.4.cloned.1.call-done, s32[1024]{0:T(1024)S(1)} %pad_clamp_fusion), kind=kCustom, calls=%fused_computation.5.clone | custom fusion | bytes 5244928 | tf_op jit(solution)/shard_map/jit(_take)/gather | solution.py:40
  317.0 5.6 fusion.4
  322.6 3.8 copy.20
  326.4 0.0 reduce-scatter.7.cloned.1.call-update
  326.4 0.0 reduce-scatter.9.cloned.1.call-start
  326.5 4.0 copy.22
  330.5 0.0 reduce-scatter.9.cloned.1.call-update
  330.5 0.0 all-gather.6.cloned.1.call-start
  330.5 118.5 %reduce-scatter.7.cloned.1.call-done = bf16[80,320]{1,0:T(8,128)(2,1)} async-done(((bf16[2560,320]{1,0:T(8,128)(2,1)}), bf16[80,320]{1,0:T(8,128)(2,1)}) %reduce-scatter.7.cloned.1.call-update) | async-done | bytes 51216
  449.0 0.9 copy.21
  450.0 118.2 %reduce-scatter.9.cloned.1.call-done = bf16[80,320]{1,0:T(8,128)(2,1)} async-done(((bf16[2560,320]{1,0:T(8,128)(2,1)}), bf16[80,320]{1,0:T(8,128)(2,1)}) %reduce-scatter.9.cloned.1.call-update) | async-done | bytes 51216
  568.1 0.9 copy.23
  569.1 0.7 copy.19
  569.9 0.0 all-gather.6.cloned.1.call-update
  569.9 75.4 %all-gather.6.cloned.1.call-done = bf16[2560,320]{1,0:T(8,128)(2,1)} async-done(((bf16[80,320]{1,0:T(8,128)(2,1)}), bf16[2560,320]{1,0:T(8,128)(2,1)}) %all-gather.6.cloned.1.call-update) | async-done | bytes 1638416 | tf_op jit(solution)/shard_map/all_gather | solution.py:60
  645.3 3.4 fusion.14
  (32 shorter events, 0.4 us)
Async XLA Ops:
  7.2 252.5 %all-gather.4.cloned.1.call-start = ((), (), s32[]{:S(2)}) async-start(), calls=%async_computation.3 | async-start | bytes 11141120 | tf_op jit(solution)/shard_map/all_gather | solution.py:30
  7.9 11.5 %copy-start.3 = (s32[128]{0:T(128)S(1)}, s32[128]{0:T(128)}, u32[]{:S(2)}) copy-start(s32[128]{0:T(128)} %param.16) | copy-start | bytes 1540
  7.9 95.6 %copy-start.2 = (s32[1,2048]{1,0:T(1,128)S(1)}, s32[1,2048]{1,0:T(1,128)}, u32[]{:S(2)}) copy-start(s32[1,2048]{1,0:T(1,128)} %param.17) | copy-start | bytes 24580
  10.3 106.0 %all-to-all-start = ((bf16[128,16,320]{0,2,1:T(8,128)(2,1)}), bf16[128,16,320]{0,2,1:T(8,128)(2,1)S(1)}, u32[]{:S(2)}, u32[]{:S(2)}) async-start(bf16[128,16,320]{0,2,1:T(8,128)(2,1)} %bitcast.3), calls=%async_computation | async-start | bytes 2621440 | tf_op jit(solution)/shard_map/all_to_all | solution.py:31
  19.4 429.6 %reduce-scatter.7.cloned.1.call-start = ((), (), s32[]{:S(2)}) async-start(), calls=%async_computation.5 | async-start | bytes 2027520
  305.2 11.8 %copy-start.1 = (f32[2560,320]{0,1:T(8,128)S(1)}, f32[2560,320]{0,1:T(8,128)}, u32[]{:S(2)}) copy-start(f32[2560,320]{0,1:T(8,128)} %fusion.1) | copy-start | bytes 9830404
  326.4 241.7 %reduce-scatter.9.cloned.1.call-start = ((), (), s32[]{:S(2)}) async-start(), calls=%async_computation.6 | async-start | bytes 2027520
  326.5 318.8 %copy-start = (bf16[512,2560]{1,0:T(8,128)(2,1)S(1)}, bf16[512,2560]{1,0:T(8,128)(2,1)}, u32[]{:S(2)}) copy-start(bf16[512,2560]{1,0:T(8,128)(2,1)} %gather_fusion) | copy-start | bytes 7864324
  330.5 314.8 %all-gather.6.cloned.1.call-start = ((), (), s32[]{:S(2)}) async-start(), calls=%async_computation.4 | async-start | bytes 2027520 | tf_op jit(solution)/shard_map/all_gather | solution.py:60
Sparse Core Ops, SparseCore 0:
  10.1 249.5 all-gather.3
  326.5 122.4 reduce-scatter.6
  454.1 113.9 reduce-scatter.8
  571.8 73.4 all-gather.5
where the time goes:
time: 656 us; the launch traced here: 655 us
  waiting for transfers between devices  446 us (68%)
  local copies, waits for them, and re-layouts  82 us (12%)
  blocking collectives  80.2 us (12%)
  matrix products  20.9 us (3%)
  between operations  14 us (2%)
  starting transfers between devices  9.18 us (1%)
    unnamed x6, waiting for transfers between devices  237 us
    all_gather x1, waiting for transfers between devices, on_device(): site_acts = lax.all_gather(activations, 'shard', axis=0, tiled=True)  133 us
    all_gather x1, blocking collectives, on_device(): site_ids = lax.all_gather(token_ids, 'shard', axis=0, tiled=True)  80.2 us
    all_gather x1, waiting for transfers between devices, on_device(): whole_merged = lax.all_gather(owned, 'site', axis=0, tiled=True)  75.4 us
    gather x4, local copies, waits for them, and re-layouts, on_device(): acts_micro = jnp.take(site_acts, picked, axis=0)  45.4 us
    dot_general x4, matrix products, on_device(): lax.dot_general(acts_micro, scaled, (((0,), (0,)), ((), ())), preferred_e...  17.5 us
  transfers between devices with their start and end apart: 5, of which 4 were waited for; matrix products, arithmetic and copies ran while one was open for 5% of the time, Pallas kernels for 0%

commit v1 on v0

v1 whole, which is shorter than its diff:
```python
import math

import jax
import jax.numpy as jnp
import numpy as np
from jax import lax
from jax.sharding import Mesh
from jax.sharding import PartitionSpec as P

HEADS = 20
HEAD_DIM = 128
MICRO = 4


epsilon = 1e-06

SITE_SUB = (("zh", 4), ("y", 4), ("c", 2))
SHARD_SUB = (("x", 4), ("zl", 4))


def count_same(site_ids):
    site_events = site_ids.shape[0]
    block_rows = math.gcd(site_events, 512)
    blocks = site_ids.reshape(site_events // block_rows, block_rows)

    def one_block(block_ids):
        return jnp.sum((block_ids[:, None] == site_ids[None, :]).astype(jnp.int32), axis=1)

    return lax.map(one_block, blocks).reshape(site_events)


def make_body(site_axes, shard_axes):
    site_names = tuple(n for n, _ in site_axes)
    site_sizes = tuple(s for _, s in site_axes)
    shard_names = tuple(n for n, _ in shard_axes)

    def gather_events(x):
        for name in reversed(shard_names):
            x = lax.all_gather(x, name, axis=0, tiled=True)
        return x

    def scatter_sites(x):
        rows = x.shape[0]
        n = len(site_sizes)
        x = x.reshape(site_sizes + (rows // math.prod(site_sizes),) + x.shape[1:])
        x = jnp.transpose(x, tuple(reversed(range(n))) + tuple(range(n, x.ndim)))
        x = x.reshape((rows,) + x.shape[n + 1 :])
        for name in reversed(site_names):
            x = lax.psum_scatter(x, name, scatter_dimension=0, tiled=True)
        return x

    def gather_sites(x):
        for name in site_names:
            x = lax.all_gather(x, name, axis=0, tiled=True)
        n = len(site_sizes)
        rows = x.shape[0]
        x = x.reshape(tuple(reversed(site_sizes)) + (rows // math.prod(site_sizes),) + x.shape[1:])
        x = jnp.transpose(x, tuple(reversed(range(n))) + tuple(range(n, x.ndim)))
        return x.reshape((rows,) + x.shape[n + 1 :])

    def on_device(activations, out_grads, theta, token_ids, assignment):
        head_cols = HEADS * HEAD_DIM
        site_ids = lax.all_gather(token_ids, shard_names, axis=0, tiled=True)
        site_acts = gather_events(activations)
        grad_cols = lax.all_to_all(out_grads, shard_names, split_axis=1, concat_axis=0, tiled=True)
        site_events = site_acts.shape[0]
        micro_rows = site_events // MICRO
        ordering = assignment[0]
        counts = count_same(site_ids)
        weights = 1.0 / counts.astype(jnp.float32)
        scaled = (grad_cols.astype(jnp.float32) * weights[:, None]).astype(jnp.bfloat16)
        position_batch = (jnp.arange(site_events, dtype=jnp.int32) // micro_rows)[None, :]
        hit = ordering[None, :] == jnp.arange(site_events, dtype=jnp.int32)[:, None]
        batch_of = jnp.sum(jnp.where(hit, position_batch, 0), axis=1)
        masked = jnp.concatenate(
            [jnp.where((batch_of == m)[:, None], scaled, jnp.zeros_like(scaled)) for m in range(MICRO)],
            axis=1,
        )
        gradients = lax.dot_general(
            site_acts, masked, (((0,), (0,)), ((), ())), preferred_element_type=jnp.float32
        )
        cols = scaled.shape[1]
        fisher = gradients[:, :cols] * gradients[:, :cols]
        for micro in range(1, MICRO):
            g = gradients[:, micro * cols : (micro + 1) * cols]
            fisher = fisher + g * g
        fisher = fisher / MICRO
        product = fisher * theta[0].astype(jnp.float32)
        both = jnp.concatenate([product.astype(jnp.bfloat16), fisher.astype(jnp.bfloat16)], axis=1)
        summed = scatter_sites(both).astype(jnp.float32)
        numerator, denominator = summed[:, :cols], summed[:, cols:]
        owned = (numerator / (denominator + epsilon)).astype(jnp.bfloat16)
        whole_merged = gather_sites(owned)
        scaling = float(head_cols) ** (-0.5)
        answers = (
            jnp.dot(site_acts, whole_merged, preferred_element_type=jnp.float32) * scaling
        ).astype(jnp.bfloat16)
        response = jnp.take(answers, ordering[:micro_rows], axis=0)
        return (owned, response)

    return on_device


def solution(mesh):
    sizes = dict(mesh.shape)
    site_ok = math.prod(s for _, s in SITE_SUB) == sizes["site"]
    shard_ok = math.prod(s for _, s in SHARD_SUB) == sizes["shard"]
    if site_ok and shard_ok:
        site_axes, shard_axes = SITE_SUB, SHARD_SUB
        shape = tuple(s for _, s in SITE_SUB + SHARD_SUB)
        names = tuple(n for n, _ in SITE_SUB + SHARD_SUB)
        use_mesh = Mesh(np.asarray(mesh.devices).reshape(shape), names)
    else:
        site_axes, shard_axes = (("site", sizes["site"]),), (("shard", sizes["shard"]),)
        use_mesh = mesh
    site = tuple(n for n, _ in site_axes)
    shard = tuple(n for n, _ in shard_axes)
    placed = (
        P(site + shard, None),
        P(site + shard, None),
        P(site, None, shard),
        P(site + shard),
        P(site, None),
    )
    return jax.shard_map(
        make_body(site_axes, shard_axes),
        mesh=use_mesh,
        in_specs=placed,
        out_specs=(P(site, shard), P(site, shard)),
        check_vma=False,
    )
```

time: 656 us -> 407 us (0.62)
  waiting for transfers between devices: 446 us -> 243 us
  local copies, waits for them, and re-layouts: 82 us -> 15 us
  other arithmetic: 3.16 us -> 14 us
  matrix products: 20.9 us -> 28.5 us
    unnamed x6, waiting for transfers between devices: 237 us -> 0.76 us
    reduce_scatter x0 -> x3, waiting for transfers between devices: none -> 106 us  [scatter_sites(): x = lax.psum_scatter(x, name, scatter_dimension=0, tiled=True)]
    all_gather x2 -> x3, waiting for transfers between devices: 208 us -> 137 us  [the longest x2 114 us: gather_events(): x = lax.all_gather(x, name, axis=0, tiled=True)]
    gather x12 -> x1, local copies, waits for them, and re-layouts: 67.6 us -> 1.94 us  [on_device(): response = jnp.take(answers, ordering[:micro_rows], axis=0)]
    unnamed x15 -> x13, local copies, waits for them, and re-layouts: 12.9 us -> 2.38 us
    dot_general x5 -> x2, matrix products: 20.9 us -> 28.5 us  [the longest x1 20.1 us: on_device(): lax.dot_general(site_acts, masked, (((0,), (0,)), ((), ())), preferred_el...]
    all_gather x1 -> x3, blocking collectives: 80.2 us -> 85.4 us  [the longest x1 54.1 us: on_device(): site_ids = lax.all_gather(token_ids, shard_names, axis=0, tiled=True)]
  transfers between devices with their start and end apart: 5 -> 7, of which waited for: 4 -> 6; matrix products, arithmetic and copies ran while one was open for 5% -> 2% of each run, Pallas kernels for 0% -> 0%
where the time goes in v1:
time: 407 us
  waiting for transfers between devices  243 us (60%)
  blocking collectives  85.4 us (21%)
  matrix products  28.5 us (7%)
  local copies, waits for them, and re-layouts  15 us (4%)
  between operations  14.4 us (4%)
  other arithmetic  14 us (3%)
  starting transfers between devices  6.09 us (1%)
    all_gather x2, waiting for transfers between devices, gather_events(): x = lax.all_gather(x, name, axis=0, tiled=True)  114 us
    reduce_scatter x3, waiting for transfers between devices, scatter_sites(): x = lax.psum_scatter(x, name, scatter_dimension=0, tiled=True)  106 us
    all_gather x1, blocking collectives, on_device(): site_ids = lax.all_gather(token_ids, shard_names, axis=0, tiled=True)  54.1 us
    all_gather x2, blocking collectives, gather_sites(): x = lax.all_gather(x, name, axis=0, tiled=True)  31.2 us
    all_gather x1, waiting for transfers between devices, gather_sites(): x = lax.all_gather(x, name, axis=0, tiled=True)  22.5 us
    dot_general x1, matrix products, on_device(): lax.dot_general(site_acts, masked, (((0,), (0,)), ((), ())), preferred_el...  20.1 us
    dot_general x1, matrix products, on_device(): jnp.dot(site_acts, whole_merged, preferred_element_type=jnp.float32)  8.45 us
  transfers between devices with their start and end apart: 7, of which 6 were waited for; matrix products, arithmetic and copies ran while one was open for 2% of the time, Pallas kernels for 0%

profile of v1, /device:TPU:1, one launch (start us, length us, event | category | flops | bytes accessed | tf_op | source)
XLA Modules:
  0.0 406.7 jit_solution(11999865053626537236)
XLA Ops:
  7.2 0.0 all-gather.5.cloned.1.call-start
  7.2 0.7 all-gather.5.cloned.1.call-update
  7.9 0.0 all-gather.7.cloned.1.call-start
  8.0 71.0 %all-gather.5.cloned.1.call-done = bf16[512,2560]{1,0:T(8,128)(2,1)} async-done(((bf16[128,2560]{1,0:T(8,128)(2,1)}), bf16[512,2560]{1,0:T(8,128)(2,1)}) %all-gather.5.cloned.1.call-update) | async-done | bytes 2621456 | tf_op jit(solution)/shard_map/all_gather | solution.py:39
  78.9 0.0 all-gather.7.cloned.1.call-update
  79.0 1.5 copy.30
  80.4 5.9 %all-to-all-start = ((bf16[128,16,320]{0,2,1:T(8,128)(2,1)}), bf16[128,16,320]{0,2,1:T(8,128)(2,1)S(1)}, u32[]{:S(2)}, u32[]{:S(2)}) async-start(bf16[128,16,320]{0,2,1:T(8,128)(2,1)} %bitcast.3), calls=%async_computation | async-start | bytes 2621440 | tf_op jit(solution)/shard_map/all_to_all | solution.py:65
  86.3 0.0 reduce-scatter.4.cloned.1.call-start
  86.4 54.1 %all-gather = s32[16,1,128]{2,1,0:T(1,128)S(1)} all-gather(s32[1,1,128]{2,1,0:T(1,128)S(1)} %bitcast.55), channel_id=1, replica_groups=mesh['zh'=4,'y'=4,'c'=2,'x'=4,'zl'=4] {'x','zl'}, dimensions={0}, use_global_device_ids=true | all-gather | bytes 8704 | tf_op jit(solution)/shard_map/all_gather | solution.py:63
  140.5 0.5 broadcast.98
  141.0 0.7 reduce.3
  141.7 2.7 while.10
  141.7 0.6 convert_reduce_fusion.2
  142.4 0.6 convert_reduce_fusion.2
  143.1 0.6 convert_reduce_fusion.2
  143.7 0.6 convert_reduce_fusion.2
  144.4 1.7 select_reduce_fusion
  146.2 0.0 all-to-all-done
  146.2 0.4 broadcast_select_fusion.3
  146.6 1.8 broadcast_select_fusion.2
  148.4 43.2 %all-gather.7.cloned.1.call-done = bf16[2048,2560]{1,0:T(8,128)(2,1)} async-done(((bf16[512,2560]{1,0:T(8,128)(2,1)}), bf16[2048,2560]{1,0:T(8,128)(2,1)}) %all-gather.7.cloned.1.call-update) | async-done | bytes 10485776 | tf_op jit(solution)/shard_map/all_gather | solution.py:39
  191.6 20.1 %convolution_bitcast_fusion = f32[2560,1280]{0,1:T(8,128)} fusion(bf16[2048,2560]{1,0:T(8,128)(2,1)} %all-gather.7.cloned.1.call-done, bf16[2048,320]{0,1:T(8,128)(2,1)} %get-tuple-element.49, bf16[2048,320]{0,1:T(8,128)(2,1)} %get-tuple-element.48, bf16[2048,320]{0,1:T(8,128)(2,1)S(1)} %get-tuple-element.47, bf16[2048,320]{0,1:T(8,128)(2,1)S(1)} %get-tuple-element.45), kind=kOutput, calls=%fused_computation.5 | convolution fusion | flops 13442744320 | bytes 28835840 | tf_op jit(solution)/shard_map/dot_general | solution.py:79
  211.7 5.6 %fusion.11 = (bf16[2560,320]{0,1:T(8,128)(2,1)S(1)}, bf16[2560,320]{0,1:T(8,128)(2,1)S(1)}) fusion(bf16[1,2560,320]{1,2,0:T(8,128)(2,1)S(1)} %copy-done, f32[2560,1280]{0,1:T(8,128)} %convolution_bitcast_fusion), kind=kLoop, calls=%fused_computation.23 | loop fusion | flops 9830400 | bytes 18022400 | tf_op jit(solution)/shard_map/convert_element_type | solution.py:89
  217.3 0.2 pad_maximum_fusion
  217.5 3.4 copy.32
  220.9 4.0 copy.33
  224.9 0.0 reduce-scatter.4.cloned.1.call-update
  224.9 0.0 reduce-scatter.6.cloned.1.call-start
  225.0 25.6 %reduce-scatter.4.cloned.1.call-done = bf16[1280,640]{1,0:T(8,128)(2,1)} async-done(((bf16[2560,640]{1,0:T(8,128)(2,1)}), bf16[1280,640]{1,0:T(8,128)(2,1)}) %reduce-scatter.4.cloned.1.call-update) | async-done | bytes 1638416 | tf_op jit(solution)/shard_map/reduce_scatter | solution.py:49
  250.6 0.0 reduce-scatter.6.cloned.1.call-update
  250.6 0.0 reduce-scatter.8.cloned.1.call-start
  250.6 36.5 %reduce-scatter.6.cloned.1.call-done = bf16[320,640]{1,0:T(8,128)(2,1)} async-done(((bf16[1280,640]{1,0:T(8,128)(2,1)}), bf16[320,640]{1,0:T(8,128)(2,1)}) %reduce-scatter.6.cloned.1.call-update) | async-done | bytes 409616 | tf_op jit(solution)/shard_map/reduce_scatter | solution.py:49
  287.2 0.0 reduce-scatter.8.cloned.1.call-update
  287.2 0.0 all-gather.9.cloned.1.call-start
  287.2 43.7 %reduce-scatter.8.cloned.1.call-done = bf16[80,640]{1,0:T(8,128)(2,1)} async-done(((bf16[320,640]{1,0:T(8,128)(2,1)}), bf16[80,640]{1,0:T(8,128)(2,1)}) %reduce-scatter.8.cloned.1.call-update) | async-done | bytes 102416 | tf_op jit(solution)/shard_map/reduce_scatter | solution.py:49
  330.9 0.9 convert_element_type.56
  331.8 0.1 fusion.16
  331.9 0.0 copy-start.2
  331.9 16.0 %all_gather.21 = bf16[320,320]{1,0:T(8,128)(2,1)S(1)} all-gather(bf16[80,320]{1,0:T(8,128)(2,1)S(1)} %fusion.16), channel_id=1, replica_groups=mesh['zh'=4,'y'=4,'c'=2,'x'=4,'zl'=4] {'zh'}, dimensions={0}, use_global_device_ids=true | all-gather | bytes 256000 | tf_op jit(solution)/shard_map/all_gather | solution.py:54
  347.9 15.2 %all_gather.22 = bf16[1280,320]{1,0:T(8,128)(2,1)} all-gather(bf16[320,320]{1,0:T(8,128)(2,1)S(1)} %all_gather.21), channel_id=1, replica_groups=mesh['zh'=4,'y'=4,'c'=2,'x'=4,'zl'=4] {'y'}, dimensions={0}, use_global_device_ids=true | all-gather | bytes 1024000 | tf_op jit(solution)/shard_map/all_gather | solution.py:54
  363.2 0.0 all-gather.9.cloned.1.call-update
  363.2 22.5 %all-gather.9.cloned.1.call-done = bf16[2560,320]{1,0:T(8,128)(2,1)} async-done(((bf16[1280,320]{1,0:T(8,128)(2,1)}), bf16[2560,320]{1,0:T(8,128)(2,1)}) %all-gather.9.cloned.1.call-update) | async-done | bytes 1638416 | tf_op jit(solution)/shard_map/all_gather | solution.py:54
  385.8 1.8 copy.34
  387.5 8.4 %fusion.14 = bf16[2048,320]{0,1:T(8,128)(2,1)S(1)} fusion(bf16[2560,320]{1,0:T(8,128)(2,1)S(1)} %bitcast.47, bf16[2048,2560]{1,0:T(8,128)(2,1)} %all-gather.7.cloned.1.call-done), kind=kOutput, calls=%fused_computation.29 | convolution fusion | flops 3356753920 | bytes 13434880 | tf_op jit(solution)/shard_map/dot_general | solution.py:96
  396.0 0.8 copy.35
  396.9 1.9 gather_fusion
  398.8 0.1 broadcast_select_fusion.4
  399.0 0.9 copy.36
  (27 shorter events, 0.3 us)
Async XLA Ops:
  7.2 71.8 %copy-start.1 = (bf16[128,5120]{1,0:T(8,128)(2,1)S(1)}, bf16[128,5120]{1,0:T(8,128)(2,1)}, u32[]{:S(2)}) copy-start(bf16[128,5120]{1,0:T(8,128)(2,1)} %param.8) | copy-start | bytes 3932164
  7.2 71.8 %all-gather.5.cloned.1.call-start = ((), (), s32[]{:S(2)}) async-start(), calls=%async_computation.4 | async-start | bytes 3276800 | tf_op jit(solution)/shard_map/all_gather | solution.py:39
  7.9 183.7 %all-gather.7.cloned.1.call-start = ((), (), s32[]{:S(2)}) async-start(), calls=%async_computation.5 | async-start | bytes 13107200 | tf_op jit(solution)/shard_map/all_gather | solution.py:39
  79.0 7.4 %copy-start.4 = (s32[128]{0:T(128)S(1)}, s32[128]{0:T(128)}, u32[]{:S(2)}) copy-start(s32[128]{0:T(128)} %param.10) | copy-start | bytes 1540
  79.0 65.5 %copy-start.3 = (s32[1,2048]{1,0:T(1,128)S(1)}, s32[1,2048]{1,0:T(1,128)}, u32[]{:S(2)}) copy-start(s32[1,2048]{1,0:T(1,128)} %param.11) | copy-start | bytes 24580
  80.4 65.8 %all-to-all-start = ((bf16[128,16,320]{0,2,1:T(8,128)(2,1)}), bf16[128,16,320]{0,2,1:T(8,128)(2,1)S(1)}, u32[]{:S(2)}, u32[]{:S(2)}) async-start(bf16[128,16,320]{0,2,1:T(8,128)(2,1)} %bitcast.3), calls=%async_computation | async-start | bytes 2621440 | tf_op jit(solution)/shard_map/all_to_all | solution.py:65
  86.3 164.3 %reduce-scatter.4.cloned.1.call-start = ((), (), s32[]{:S(2)}) async-start(), calls=%async_computation.6 | async-start | bytes 4915200 | tf_op jit(solution)/shard_map/reduce_scatter | solution.py:49
  191.6 20.1 %copy-start = (bf16[1,2560,320]{1,2,0:T(8,128)(2,1)S(1)}, bf16[1,2560,320]{1,2,0:T(8,128)(2,1)}, u32[]{:S(2)}) copy-start(bf16[1,2560,320]{1,2,0:T(8,128)(2,1)} %param.9) | copy-start | bytes 4915204
  224.9 62.2 %reduce-scatter.6.cloned.1.call-start = ((), (), s32[]{:S(2)}) async-start(), calls=%async_computation.7 | async-start | bytes 2048000 | tf_op jit(solution)/shard_map/reduce_scatter | solution.py:49
  250.6 80.3 %reduce-scatter.8.cloned.1.call-start = ((), (), s32[]{:S(2)}) async-start(), calls=%async_computation.8 | async-start | bytes 512000 | tf_op jit(solution)/shard_map/reduce_scatter | solution.py:49
  287.2 98.6 %all-gather.9.cloned.1.call-start = ((), (), s32[]{:S(2)}) async-start(), calls=%async_computation.9 | async-start | bytes 2949120 | tf_op jit(solution)/shard_map/all_gather | solution.py:54
  331.9 64.1 %copy-start.2 = (bf16[80,320]{1,0:T(8,128)(2,1)}, bf16[80,320]{1,0:T(8,128)(2,1)S(1)}, u32[]{:S(2)}) copy-start(bf16[80,320]{1,0:T(8,128)(2,1)S(1)} %fusion.16) | copy-start | bytes 153604
Sparse Core Ops, SparseCore 0:
  10.1 68.7 all-gather.4
  81.0 110.5 all-gather.6
  225.0 25.4 reduce-scatter.3
  253.5 33.6 reduce-scatter.5
  289.8 41.0 reduce-scatter.7
  363.3 22.4 all-gather.8

commit v2 on v1

--- a/solution.py
+++ b/solution.py
@@ -16,6 +16,7 @@
 
 SITE_SUB = (("zh", 4), ("y", 4), ("c", 2))
 SHARD_SUB = (("x", 4), ("zl", 4))
+SCATTER_STAGES = (("y", "c"), ("zh",))
 
 
 def count_same(site_ids):
@@ -29,10 +30,24 @@
     return lax.map(one_block, blocks).reshape(site_events)
 
 
-def make_body(site_axes, shard_axes):
+def make_body(site_axes, shard_axes, scatter_stages):
     site_names = tuple(n for n, _ in site_axes)
     site_sizes = tuple(s for _, s in site_axes)
     shard_names = tuple(n for n, _ in shard_axes)
+    position_names = tuple(n for stage in scatter_stages for n in stage)
+    position_axes = tuple(site_names.index(n) for n in position_names)
+    n_sub = len(site_sizes)
+
+    def to_position_order(x, axis):
+        shape = x.shape
+        block = shape[axis] // math.prod(site_sizes)
+        x = x.reshape(shape[:axis] + site_sizes + (block,) + shape[axis + 1 :])
+        order = (
+            tuple(range(axis))
+            + tuple(axis + a for a in position_axes)
+            + tuple(range(axis + n_sub, x.ndim))
+        )
+        return jnp.transpose(x, order).reshape(shape)
 
     def gather_events(x):
         for name in reversed(shard_names):
@@ -40,29 +55,21 @@
         return x
 
     def scatter_sites(x):
-        rows = x.shape[0]
-        n = len(site_sizes)
-        x = x.reshape(site_sizes + (rows // math.prod(site_sizes),) + x.shape[1:])
-        x = jnp.transpose(x, tuple(reversed(range(n))) + tuple(range(n, x.ndim)))
-        x = x.reshape((rows,) + x.shape[n + 1 :])
-        for name in reversed(site_names):
-            x = lax.psum_scatter(x, name, scatter_dimension=0, tiled=True)
+        for stage in scatter_stages:
+            x = lax.psum_scatter(x, stage, scatter_dimension=0, tiled=True)
         return x
 
     def gather_sites(x):
-        for name in site_names:
-            x = lax.all_gather(x, name, axis=0, tiled=True)
-        n = len(site_sizes)
-        rows = x.shape[0]
-        x = x.reshape(tuple(reversed(site_sizes)) + (rows // math.prod(site_sizes),) + x.shape[1:])
-        x = jnp.transpose(x, tuple(reversed(range(n))) + tuple(range(n, x.ndim)))
-        return x.reshape((rows,) + x.shape[n + 1 :])
+        for stage in reversed(scatter_stages):
+            x = lax.all_gather(x, stage, axis=0, tiled=True)
+        return x
 
     def on_device(activations, out_grads, theta, token_ids, assignment):
         head_cols = HEADS * HEAD_DIM
         site_ids = lax.all_gather(token_ids, shard_names, axis=0, tiled=True)
-        site_acts = gather_events(activations)
+        site_acts = gather_events(to_position_order(activations, 1))
         grad_cols = lax.all_to_all(out_grads, shard_names, split_axis=1, concat_axis=0, tiled=True)
+        theta_rows = to_position_order(theta[0], 0)
         site_events = site_acts.shape[0]
         micro_rows = site_events // MICRO
         ordering = assignment[0]
@@ -85,17 +92,17 @@
             g = gradients[:, micro * cols : (micro + 1) * cols]
             fisher = fisher + g * g
         fisher = fisher / MICRO
-        product = fisher * theta[0].astype(jnp.float32)
+        product = fisher * theta_rows.astype(jnp.float32)
         both = jnp.concatenate([product.astype(jnp.bfloat16), fisher.astype(jnp.bfloat16)], axis=1)
         summed = scatter_sites(both).astype(jnp.float32)
         numerator, denominator = summed[:, :cols], summed[:, cols:]
         owned = (numerator / (denominator + epsilon)).astype(jnp.bfloat16)
         whole_merged = gather_sites(owned)
         scaling = float(head_cols) ** (-0.5)
-        answers = (
-            jnp.dot(site_acts, whole_merged, preferred_element_type=jnp.float32) * scaling
+        probe = jnp.take(site_acts, ordering[:micro_rows], axis=0)
+        response = (
+            jnp.dot(probe, whole_merged, preferred_element_type=jnp.float32) * scaling
         ).astype(jnp.bfloat16)
-        response = jnp.take(answers, ordering[:micro_rows], axis=0)
         return (owned, response)
 
     return on_device
@@ -107,11 +114,13 @@
     shard_ok = math.prod(s for _, s in SHARD_SUB) == sizes["shard"]
     if site_ok and shard_ok:
         site_axes, shard_axes = SITE_SUB, SHARD_SUB
+        scatter_stages = SCATTER_STAGES
         shape = tuple(s for _, s in SITE_SUB + SHARD_SUB)
         names = tuple(n for n, _ in SITE_SUB + SHARD_SUB)
         use_mesh = Mesh(np.asarray(mesh.devices).reshape(shape), names)
     else:
         site_axes, shard_axes = (("site", sizes["site"]),), (("shard", sizes["shard"]),)
+        scatter_stages = (("site",),)
         use_mesh = mesh
     site = tuple(n for n, _ in site_axes)
     shard = tuple(n for n, _ in shard_axes)
@@ -123,7 +132,7 @@
         P(site, None),
     )
     return jax.shard_map(
-        make_body(site_axes, shard_axes),
+        make_body(site_axes, shard_axes, scatter_stages),
         mesh=use_mesh,
         in_specs=placed,
         out_specs=(P(site, shard), P(site, shard)),

time: 407 us -> 373 us (0.916)
  waiting for transfers between devices: 243 us -> 211 us
  local copies, waits for them, and re-layouts: 15 us -> 29.4 us
  blocking collectives: 85.4 us -> 71.2 us
  matrix products: 28.5 us -> 24.2 us
    reduce_scatter x3 -> x0, waiting for transfers between devices: 106 us -> none  [scatter_sites(): x = lax.psum_scatter(x, name, scatter_dimension=0, tiled=True)]
    unnamed x6 -> x7, waiting for transfers between devices: 0.76 us -> 89.6 us
    all_gather x2, waiting for transfers between devices: 114 us -> 99.7 us  [gather_events(): x = lax.all_gather(x, name, axis=0, tiled=True)]
    all_gather x2 -> x1, blocking collectives: 31.2 us -> 17.1 us  [gather_sites(): x = lax.all_gather(x, stage, axis=0, tiled=True)]
    unnamed x13 -> x15, local copies, waits for them, and re-layouts: 2.38 us -> 11.1 us
    gather x1, local copies, waits for them, and re-layouts: 1.94 us -> 10.5 us  [on_device(): probe = jnp.take(site_acts, ordering[:micro_rows], axis=0)]
    convert_element_type x1 -> x2, local copies, waits for them, and re-layouts: 0.85 us -> 5.86 us  [on_device(): product = fisher * theta_rows.astype(jnp.float32)]
    dot_general x1, matrix products: 8.45 us -> 3.44 us  [on_device(): jnp.dot(probe, whole_merged, preferred_element_type=jnp.float32) * scaling]
  transfers between devices with their start and end apart: 7 -> 6, of which waited for: 6 -> 5; matrix products, arithmetic and copies ran while one was open for 2% -> 9% of each run, Pallas kernels for 0% -> 0%
where the time goes in v2:
time: 373 us; the launch traced here: 372 us
  waiting for transfers between devices  211 us (57%)
  blocking collectives  71.2 us (19%)
  local copies, waits for them, and re-layouts  29.4 us (8%)
  matrix products  24.2 us (6%)
  other arithmetic  15.9 us (4%)
  between operations  14 us (4%)
  starting transfers between devices  6.1 us (2%)
    all_gather x2, waiting for transfers between devices, gather_events(): x = lax.all_gather(x, name, axis=0, tiled=True)  99.7 us
    unnamed x7, waiting for transfers between devices  89.6 us
    all_gather x1, blocking collectives, on_device(): site_ids = lax.all_gather(token_ids, shard_names, axis=0, tiled=True)  54.1 us
    all_gather x1, waiting for transfers between devices, gather_sites(): x = lax.all_gather(x, stage, axis=0, tiled=True)  22.1 us
    dot_general x1, matrix products, on_device(): lax.dot_general(site_acts, masked, (((0,), (0,)), ((), ())), preferred_el...  20.7 us
    all_gather x1, blocking collectives, gather_sites(): x = lax.all_gather(x, stage, axis=0, tiled=True)  17.1 us
    unnamed x15, local copies, waits for them, and re-layouts  11.1 us
    gather x1, local copies, waits for them, and re-layouts, on_device(): probe = jnp.take(site_acts, ordering[:micro_rows], axis=0)  10.5 us
  transfers between devices with their start and end apart: 6, of which 5 were waited for; matrix products, arithmetic and copies ran while one was open for 9% of the time, Pallas kernels for 0%

profile of v2, /device:TPU:1, one launch (start us, length us, event | category | flops | bytes accessed | tf_op | source)
XLA Modules:
  0.0 372.4 jit_solution(10758061057035203634)
XLA Ops:
  7.2 0.0 all-gather.5.cloned.1.call-start
  7.2 1.4 copy.31
  8.6 0.0 copy-start
  8.7 1.1 copy.33
  9.8 0.0 all-gather.5.cloned.1.call-update
  9.8 0.0 all-gather.7.cloned.1.call-start
  9.9 69.1 %all-gather.5.cloned.1.call-done = bf16[512,2560]{1,0:T(8,128)(2,1)} async-done(((bf16[128,2560]{1,0:T(8,128)(2,1)}), bf16[512,2560]{1,0:T(8,128)(2,1)}) %all-gather.5.cloned.1.call-update) | async-done | bytes 2621456 | tf_op jit(solution)/shard_map/all_gather | solution.py:54
  78.9 0.0 all-gather.7.cloned.1.call-update
  78.9 0.0 copy-done
  79.0 0.0 copy-start.3
  79.0 1.5 copy.29
  80.5 5.9 %all-to-all-start = ((bf16[128,16,320]{0,2,1:T(8,128)(2,1)}), bf16[128,16,320]{0,2,1:T(8,128)(2,1)}, u32[]{:S(2)}, u32[]{:S(2)}) async-start(bf16[128,16,320]{0,2,1:T(8,128)(2,1)} %bitcast.3), calls=%async_computation | async-start | bytes 2621440 | tf_op jit(solution)/shard_map/all_to_all | solution.py:71
  86.4 0.0 reduce-scatter.7.cloned.1.call-start
  86.5 54.1 %all-gather = s32[16,1,128]{2,1,0:T(1,128)S(1)} all-gather(s32[1,1,128]{2,1,0:T(1,128)S(1)} %bitcast.52), channel_id=1, replica_groups=mesh['zh'=4,'y'=4,'c'=2,'x'=4,'zl'=4] {'x','zl'}, dimensions={0}, use_global_device_ids=true | all-gather | bytes 8704 | tf_op jit(solution)/shard_map/all_gather | solution.py:69
  140.6 0.5 broadcast.96
  141.1 0.7 reduce.3
  141.8 2.7 while.10
  141.8 0.6 convert_reduce_fusion.2
  142.5 0.6 convert_reduce_fusion.2
  143.1 0.6 convert_reduce_fusion.2
  143.8 0.6 convert_reduce_fusion.2
  144.5 3.6 copy.34
  148.1 0.4 convert_bitcast_fusion
  148.5 2.2 copy.35
  150.7 3.7 copy.36
  154.4 1.7 select_reduce_fusion
  156.2 0.0 all-to-all-done
  156.2 2.8 broadcast_select_fusion.3
  158.9 2.0 broadcast_select_fusion.2
  161.0 30.7 %all-gather.7.cloned.1.call-done = bf16[2048,2560]{1,0:T(8,128)(2,1)} async-done(((bf16[512,2560]{1,0:T(8,128)(2,1)}), bf16[2048,2560]{1,0:T(8,128)(2,1)}) %all-gather.7.cloned.1.call-update) | async-done | bytes 10485776 | tf_op jit(solution)/shard_map/all_gather | solution.py:54
  191.6 20.7 %convolution_bitcast_fusion = f32[2560,1280]{0,1:T(8,128)} fusion(bf16[2048,2560]{1,0:T(8,128)(2,1)} %all-gather.7.cloned.1.call-done, bf16[2048,320]{0,1:T(8,128)(2,1)} %get-tuple-element.47, bf16[2048,320]{0,1:T(8,128)(2,1)} %get-tuple-element.46, bf16[2048,320]{0,1:T(8,128)(2,1)} %get-tuple-element.45, bf16[2048,320]{0,1:T(8,128)(2,1)} %get-tuple-element.43), kind=kOutput, calls=%fused_computation.5 | convolution fusion | flops 13442744320 | bytes 28835840 | tf_op jit(solution)/shard_map/dot_general | solution.py:86
  212.4 5.7 %multiply_convert_fusion = (bf16[2560,320]{0,1:T(8,128)(2,1)S(1)}, bf16[2560,320]{0,1:T(8,128)(2,1)S(1)}) fusion(f32[2560,320]{0,1:T(8,128)S(1)} %copy.36, f32[2560,1280]{0,1:T(8,128)} %convolution_bitcast_fusion), kind=kLoop, calls=%fused_computation.23 | loop fusion | flops 9011200 | bytes 19660800 | tf_op jit(solution)/shard_map/convert_element_type | solution.py:96
  218.1 0.2 pad_maximum_fusion
  218.3 3.4 copy.39
  221.7 0.0 reduce-scatter.7.cloned.1.call-update
  221.7 0.0 reduce-scatter.9.cloned.1.call-start
  221.8 44.8 %reduce-scatter.7.cloned.1.call-done = bf16[320,640]{1,0:T(8,128)(2,1)} async-done(((bf16[2560,640]{1,0:T(8,128)(2,1)}), bf16[320,640]{1,0:T(8,128)(2,1)}) %reduce-scatter.7.cloned.1.call-update) | async-done | bytes 409616
  266.5 0.0 reduce-scatter.9.cloned.1.call-update
  266.5 0.0 all-gather.9.cloned.1.call-start
  266.6 44.8 %reduce-scatter.9.cloned.1.call-done = bf16[80,640]{1,0:T(8,128)(2,1)} async-done(((bf16[320,640]{1,0:T(8,128)(2,1)}), bf16[80,640]{1,0:T(8,128)(2,1)}) %reduce-scatter.9.cloned.1.call-update) | async-done | bytes 102416
  311.3 1.1 copy.42
  312.5 0.1 copy.38
  312.6 0.0 copy-start.1
  312.6 17.1 %all_gather.18 = bf16[320,320]{1,0:T(8,128)(2,1)} all-gather(bf16[80,320]{1,0:T(8,128)(2,1)S(1)} %copy.38), channel_id=1, replica_groups=mesh['zh'=4,'y'=4,'c'=2,'x'=4,'zl'=4] {'zh'}, dimensions={0}, use_global_device_ids=true | all-gather | bytes 256000 | tf_op jit(solution)/shard_map/all_gather | solution.py:64
  329.7 0.0 all-gather.9.cloned.1.call-update
  329.8 10.5 %gather_fusion = bf16[512,2560]{1,0:T(8,128)(2,1)S(1)} fusion(bf16[2048,2560]{1,0:T(8,128)(2,1)} %all-gather.7.cloned.1.call-done, s32[1024]{0:T(1024)S(1)} %pad_clamp_fusion), kind=kCustom, calls=%fused_computation | custom fusion | bytes 5244928 | tf_op jit(solution)/shard_map/jit(_take)/gather | solution.py:102
  340.3 22.1 %all-gather.9.cloned.1.call-done = bf16[2560,320]{1,0:T(8,128)(2,1)} async-done(((bf16[320,320]{1,0:T(8,128)(2,1)}), bf16[2560,320]{1,0:T(8,128)(2,1)}) %all-gather.9.cloned.1.call-update) | async-done | bytes 1638416 | tf_op jit(solution)/shard_map/all_gather | solution.py:64
  362.5 3.4 fusion.19
  (25 shorter events, 0.4 us)
Async XLA Ops:
  7.2 71.8 %all-gather.5.cloned.1.call-start = ((), (), s32[]{:S(2)}) async-start(), calls=%async_computation.3 | async-start | bytes 3276800 | tf_op jit(solution)/shard_map/all_gather | solution.py:54
  8.6 70.3 %copy-start = (bf16[128,5120]{1,0:T(8,128)(2,1)S(1)}, bf16[128,5120]{1,0:T(8,128)(2,1)}, u32[]{:S(2)}) copy-start(bf16[128,5120]{1,0:T(8,128)(2,1)} %param.8) | copy-start | bytes 3932164
  9.8 181.8 %all-gather.7.cloned.1.call-start = ((), (), s32[]{:S(2)}) async-start(), calls=%async_computation.4 | async-start | bytes 13107200 | tf_op jit(solution)/shard_map/all_gather | solution.py:54
  79.0 7.5 %copy-start.3 = (s32[128]{0:T(128)S(1)}, s32[128]{0:T(128)}, u32[]{:S(2)}) copy-start(s32[128]{0:T(128)} %param.10) | copy-start | bytes 1540
  80.5 75.7 %all-to-all-start = ((bf16[128,16,320]{0,2,1:T(8,128)(2,1)}), bf16[128,16,320]{0,2,1:T(8,128)(2,1)}, u32[]{:S(2)}, u32[]{:S(2)}) async-start(bf16[128,16,320]{0,2,1:T(8,128)(2,1)} %bitcast.3), calls=%async_computation | async-start | bytes 2621440 | tf_op jit(solution)/shard_map/all_to_all | solution.py:71
  86.4 180.1 %reduce-scatter.7.cloned.1.call-start = ((), (), s32[]{:S(2)}) async-start(), calls=%async_computation.6 | async-start | bytes 3686400
  150.7 3.7 copy-start.2
  221.7 89.6 %reduce-scatter.9.cloned.1.call-start = ((), (), s32[]{:S(2)}) async-start(), calls=%async_computation.7 | async-start | bytes 512000
  266.5 95.9 %all-gather.9.cloned.1.call-start = ((), (), s32[]{:S(2)}) async-start(), calls=%async_computation.5 | async-start | bytes 2211840 | tf_op jit(solution)/shard_map/all_gather | solution.py:64
  312.6 27.8 %copy-start.1 = (bf16[80,320]{1,0:T(8,128)(2,1)}, bf16[80,320]{1,0:T(8,128)(2,1)S(1)}, u32[]{:S(2)}) copy-start(bf16[80,320]{1,0:T(8,128)(2,1)S(1)} %copy.38) | copy-start | bytes 153604
Sparse Core Ops, SparseCore 0:
  10.1 68.7 all-gather.4
  81.0 110.5 all-gather.6
  221.8 44.6 reduce-scatter.6
  269.4 41.8 reduce-scatter.8
  329.9 32.5 all-gather.8

commit v3 on v2

--- a/solution.py
+++ b/solution.py
@@ -17,6 +17,7 @@
 SITE_SUB = (("zh", 4), ("y", 4), ("c", 2))
 SHARD_SUB = (("x", 4), ("zl", 4))
 SCATTER_STAGES = (("y", "c"), ("zh",))
+SHARD_KINDS = ("ring4", "line")
 
 
 def count_same(site_ids):
@@ -30,7 +31,60 @@
     return lax.map(one_block, blocks).reshape(site_events)
 
 
-def make_body(site_axes, shard_axes, scatter_stages):
+def place_blocks(parts, n, rows):
+    shape = ((n + 1) * rows,) + parts[0][0].shape[1:]
+    out = jnp.zeros(shape, parts[0][0].dtype)
+    for value, block in parts:
+        start = (block * rows,) + (0,) * (value.ndim - 1)
+        out = lax.dynamic_update_slice(out, value, start)
+    return out[: n * rows]
+
+
+def line_gather(xs, name, n):
+    i = lax.axis_index(name)
+    rows = xs[0].shape[0]
+    right, left = [xs], [xs]
+    for step in range(1, n):
+        to_right = [(k, k + 1) for k in range(step - 1, n - 1)]
+        to_left = [(k, k - 1) for k in range(1, n - step + 1)]
+        right.append(tuple(lax.ppermute(x, name, to_right) for x in right[-1]))
+        left.append(tuple(lax.ppermute(x, name, to_left) for x in left[-1]))
+    outs = []
+    for a in range(len(xs)):
+        parts = [(xs[a], i)]
+        for step in range(1, n):
+            parts.append((right[step][a], jnp.where(i - step >= 0, i - step, n)))
+            parts.append((left[step][a], jnp.where(i + step <= n - 1, i + step, n)))
+        outs.append(place_blocks(parts, n, rows))
+    return tuple(outs)
+
+
+def ring4_gather(xs, name):
+    n = 4
+    i = lax.axis_index(name)
+    rows = xs[0].shape[0]
+    half = rows // 2
+    fw = [(k, (k + 1) % n) for k in range(n)]
+    bw = [(k, (k - 1) % n) for k in range(n)]
+    from_left = tuple(lax.ppermute(x, name, fw) for x in xs)
+    from_right = tuple(lax.ppermute(x, name, bw) for x in xs)
+    far_first = tuple(lax.ppermute(x[:half], name, fw) for x in from_left)
+    far_second = tuple(lax.ppermute(x[half:], name, bw) for x in from_right)
+    outs = []
+    for a in range(len(xs)):
+        shape = (n * rows,) + xs[a].shape[1:]
+        out = jnp.zeros(shape, xs[a].dtype)
+        zeros = (0,) * (xs[a].ndim - 1)
+        out = lax.dynamic_update_slice(out, xs[a], (i * rows,) + zeros)
+        out = lax.dynamic_update_slice(out, from_left[a], (((i + n - 1) % n) * rows,) + zeros)
+        out = lax.dynamic_update_slice(out, from_right[a], (((i + 1) % n) * rows,) + zeros)
+        out = lax.dynamic_update_slice(out, far_first[a], (((i + 2) % n) * rows,) + zeros)
+        out = lax.dynamic_update_slice(out, far_second[a], (((i + 2) % n) * rows + half,) + zeros)
+        outs.append(out)
+    return tuple(outs)
+
+
+def make_body(site_axes, shard_axes, shard_kinds, scatter_stages):
     site_names = tuple(n for n, _ in site_axes)
     site_sizes = tuple(s for _, s in site_axes)
     shard_names = tuple(n for n, _ in shard_axes)
@@ -49,10 +103,15 @@
         )
         return jnp.transpose(x, order).reshape(shape)
 
-    def gather_events(x):
-        for name in reversed(shard_names):
-            x = lax.all_gather(x, name, axis=0, tiled=True)
-        return x
+    def gather_events(xs):
+        for (name, size), kind in zip(reversed(shard_axes), reversed(shard_kinds)):
+            if kind == "line":
+                xs = line_gather(xs, name, size)
+            elif kind == "ring4":
+                xs = ring4_gather(xs, name)
+            else:
+                xs = tuple(lax.all_gather(x, name, axis=0, tiled=True) for x in xs)
+        return xs
 
     def scatter_sites(x):
         for stage in scatter_stages:
@@ -66,8 +125,7 @@
 
     def on_device(activations, out_grads, theta, token_ids, assignment):
         head_cols = HEADS * HEAD_DIM
-        site_ids = lax.all_gather(token_ids, shard_names, axis=0, tiled=True)
-        site_acts = gather_events(to_position_order(activations, 1))
+        site_acts, site_ids = gather_events((to_position_order(activations, 1), token_ids))
         grad_cols = lax.all_to_all(out_grads, shard_names, split_axis=1, concat_axis=0, tiled=True)
         theta_rows = to_position_order(theta[0], 0)
         site_events = site_acts.shape[0]
@@ -115,12 +173,14 @@
     if site_ok and shard_ok:
         site_axes, shard_axes = SITE_SUB, SHARD_SUB
         scatter_stages = SCATTER_STAGES
+        shard_kinds = SHARD_KINDS
         shape = tuple(s for _, s in SITE_SUB + SHARD_SUB)
         names = tuple(n for n, _ in SITE_SUB + SHARD_SUB)
         use_mesh = Mesh(np.asarray(mesh.devices).reshape(shape), names)
     else:
         site_axes, shard_axes = (("site", sizes["site"]),), (("shard", sizes["shard"]),)
         scatter_stages = (("site",),)
+        shard_kinds = ("collective",)
         use_mesh = mesh
     site = tuple(n for n, _ in site_axes)
     shard = tuple(n for n, _ in shard_axes)
@@ -132,7 +192,7 @@
         P(site, None),
     )
     return jax.shard_map(
-        make_body(site_axes, shard_axes, scatter_stages),
+        make_body(site_axes, shard_axes, shard_kinds, scatter_stages),
         mesh=use_mesh,
         in_specs=placed,
         out_specs=(P(site, shard), P(site, shard)),

time: 373 us -> 400 us (1.072)
  blocking collectives: 71.2 us -> 16.4 us
  starting transfers between devices: 6.1 us -> 53.6 us
  local copies, waits for them, and re-layouts: 29.4 us -> 58.4 us
  waiting for transfers between devices: 211 us -> 219 us
    ppermute x0 -> x20, waiting for transfers between devices: none -> 102 us  [the longest x6 57.1 us: line_gather(): left.append(tuple((lax.ppermute(x, name, to_left) for x in left[-1])))]
    all_gather x2 -> x0, waiting for transfers between devices: 99.7 us -> none  [gather_events(): x = lax.all_gather(x, name, axis=0, tiled=True)]
    all_gather x1 -> x0, blocking collectives: 54.1 us -> none  [on_device(): site_ids = lax.all_gather(token_ids, shard_names, axis=0, tiled=True)]
    ppermute x0 -> x20, starting transfers between devices: none -> 45.6 us  [the longest x6 11.9 us: line_gather(): right.append(tuple((lax.ppermute(x, name, to_right) for x in right[-1])))]
    dynamic_update_slice x0 -> x22, local copies, waits for them, and re-layouts: none -> 15.6 us  [the longest x2 3.69 us: ring4_gather(): lax.dynamic_update_slice(out, from_left[a], ((i + n - 1) % n * rows,) + z...]
    slice x0 -> x6, local copies, waits for them, and re-layouts: none -> 7.77 us  [the longest x2 2.75 us: place_blocks(): return out[:n * rows]]
    broadcast_in_dim x0 -> x3, local copies, waits for them, and re-layouts: none -> 4.81 us  [the longest x1 4.59 us: ring4_gather(): out = jnp.zeros(shape, xs[a].dtype)]
    unnamed x7 -> x5, waiting for transfers between devices: 89.6 us -> 94 us
  transfers between devices with their start and end apart: 6 -> 24, of which waited for: 5 -> 11; matrix products, arithmetic and copies ran while one was open for 9% -> 15% of each run, Pallas kernels for 0% -> 0%
where the time goes in v3:
time: 400 us; the launch traced here: 399 us
  waiting for transfers between devices  219 us (55%)
  local copies, waits for them, and re-layouts  58.4 us (15%)
  starting transfers between devices  53.6 us (13%)
  matrix products  22.7 us (6%)
  blocking collectives  16.4 us (4%)
  between operations  14.4 us (4%)
  other arithmetic  14.3 us (4%)
    unnamed x5, waiting for transfers between devices  94 us
    ppermute x6, waiting for transfers between devices, line_gather(): left.append(tuple((lax.ppermute(x, name, to_left) for x in left[-1])))  57.1 us
    ppermute x2, waiting for transfers between devices, ring4_gather(): from_left = tuple((lax.ppermute(x, name, fw) for x in xs))  31.4 us
    all_gather x1, waiting for transfers between devices, gather_sites(): x = lax.all_gather(x, stage, axis=0, tiled=True)  23.3 us
    dot_general x1, matrix products, on_device(): lax.dot_general(site_acts, masked, (((0,), (0,)), ((), ())), preferred_el...  19.2 us
    all_gather x1, blocking collectives, gather_sites(): x = lax.all_gather(x, stage, axis=0, tiled=True)  16.4 us
    ppermute x2, waiting for transfers between devices, ring4_gather(): far_first = tuple((lax.ppermute(x[:half], name, fw) for x in from_left))  12.4 us
    ppermute x6, starting transfers between devices, line_gather(): right.append(tuple((lax.ppermute(x, name, to_right) for x in right[-1])))  11.9 us
  transfers between devices with their start and end apart: 24, of which 11 were waited for; matrix products, arithmetic and copies ran while one was open for 15% of the time, Pallas kernels for 0%

profile of v3, /device:TPU:1, one launch (start us, length us, event | category | flops | bytes accessed | tf_op | source)
XLA Modules:
  0.0 399.3 jit_solution(3388844073413372899)
XLA Ops:
  7.2 1.5 copy.33
  9.0 5.2 %collective-permute-start = (bf16[128,2560]{1,0:T(8,128)(2,1)S(1)}, bf16[128,2560]{1,0:T(8,128)(2,1)}, u32[]{:S(2)}, u32[]{:S(2)}) collective-permute-start(bf16[128,2560]{1,0:T(8,128)(2,1)S(1)} %copy.35), channel_id=1, source_target_pairs={{0,1},{1,2},{2,3},{4,5},{5,6},{6,7},{8,9},{9,10},{10,11},{12,13},{... | collective-permute-start | bytes 1966088 | tf_op jit(solution)/shard_map/ppermute | solution.py:50
  15.5 4.0 collective-permute-start.10
  19.5 1.3 collective-permute-start.11
  20.8 1.5 copy.38
  22.3 7.9 %all-to-all-start = ((bf16[128,16,320]{0,2,1:T(8,128)(2,1)}), bf16[128,16,320]{0,2,1:T(8,128)(2,1)}, u32[]{:S(2)}, u32[]{:S(2)}) async-start(bf16[128,16,320]{0,2,1:T(8,128)(2,1)} %bitcast.6), calls=%async_computation | async-start | bytes 2621440 | tf_op jit(solution)/shard_map/all_to_all | solution.py:129
  30.3 3.6 copy.40
  34.9 1.3 collective-permute-start.3
  38.2 28.7 %collective-permute-done.3 = bf16[128,2560]{1,0:T(8,128)(2,1)S(1)} collective-permute-done((bf16[128,2560]{1,0:T(8,128)(2,1)S(1)}, bf16[128,2560]{1,0:T(8,128)(2,1)S(1)}, u32[]{:S(2)}, u32[]{:S(2)}) %collective-permute-start.3) | collective-permute-done | bytes 655392 | tf_op jit(solution)/shard_map/ppermute | solution.py:51
  66.9 1.3 collective-permute-start.5
  68.3 22.4 %collective-permute-done.5 = bf16[128,2560]{1,0:T(8,128)(2,1)S(1)} collective-permute-done((bf16[128,2560]{1,0:T(8,128)(2,1)S(1)}, bf16[128,2560]{1,0:T(8,128)(2,1)S(1)}, u32[]{:S(2)}, u32[]{:S(2)}) %collective-permute-start.5) | collective-permute-done | bytes 655392 | tf_op jit(solution)/shard_map/ppermute | solution.py:51
  90.8 4.6 %broadcast_in_dim.70 = bf16[2048,2560]{1,0:T(8,128)(2,1)} broadcast(bf16[]{:T(256)} %constant.96.clone.1), dimensions={} | broadcast | bytes 10485762 | tf_op jit(solution)/shard_map/broadcast_in_dim | solution.py:76
  95.4 2.7 fusion.32
  98.0 2.4 collective-permute-start.6
  100.4 4.1 %collective-permute-start.7 = (bf16[512,2560]{1,0:T(8,128)(2,1)}, bf16[512,2560]{1,0:T(8,128)(2,1)}, u32[]{:S(2)}, u32[]{:S(2)}) collective-permute-start(bf16[512,2560]{1,0:T(8,128)(2,1)} %get-tuple-element.45), channel_id=1, source_target_pairs={{0,12},{4,0},{8,4},{12,8},{1,13},{5,1},{9,5},{13,9},{2,14},{6,2},{... | collective-permute-start | bytes 7864328 | tf_op jit(solution)/shard_map/ppermute | solution.py:70
  104.5 1.7 select_reduce_fusion
  106.3 2.3 convert_bitcast_fusion
  109.2 1.3 collective-permute-start.13
  111.2 3.9 collective-permute-done.13
  115.2 1.3 collective-permute-start.15
  117.7 2.1 collective-permute-done.15
  120.1 1.9 collective-permute-start.16
  122.0 4.6 %collective-permute-start.17 = (s32[512]{0:T(512)S(1)}, s32[512]{0:T(512)S(1)}, u32[]{:S(2)}, u32[]{:S(2)}) collective-permute-start(s32[512]{0:T(512)S(1)} %get-tuple-element.54), channel_id=1, source_target_pairs={{0,12},{4,0},{8,4},{12,8},{1,13},{5,1},{9,5},{13,9},{2,14},{6,2},{... | collective-permute-start | bytes 6152 | tf_op jit(solution)/shard_map/ppermute | solution.py:70
  126.6 31.4 %collective-permute-done.16 = s32[512]{0:T(512)S(1)} collective-permute-done((s32[512]{0:T(512)S(1)}, s32[512]{0:T(512)S(1)}, u32[]{:S(2)}, u32[]{:S(2)}) %collective-permute-start.16) | collective-permute-done | bytes 2080 | tf_op jit(solution)/shard_map/ppermute | solution.py:69
  158.0 1.9 collective-permute-start.18
  160.2 4.4 %collective-permute-start.19 = (s32[256]{0:T(256)S(1)}, s32[256]{0:T(256)S(1)}, u32[]{:S(2)}, u32[]{:S(2)}) collective-permute-start(s32[256]{0:T(256)S(1)} %slice.50), channel_id=1, source_target_pairs={{0,12},{4,0},{8,4},{12,8},{1,13},{5,1},{9,5},{13,9},{2,14},{6,2},{... | collective-permute-start | bytes 3080 | tf_op jit(solution)/shard_map/ppermute | solution.py:72
  164.6 4.4 %copy.41 = f32[4,2,4,80,320]{4,3,2,1,0:T(8,128)} copy(f32[4,2,4,80,320]{4,3,1,0,2:T(8,128)} %convert_bitcast_fusion) | data formatting | bytes 6553600 | tf_op jit(solution)/shard_map/convert_element_type | solution.py:153
  169.0 3.6 copy.42
  173.6 2.7 while.10
  176.3 2.5 slice.63
  178.7 1.9 collective-permute-start.8
  180.7 2.5 slice.64
  183.2 4.7 %collective-permute-start.9 = (bf16[256,2560]{1,0:T(8,128)(2,1)}, bf16[256,2560]{1,0:T(8,128)(2,1)}, u32[]{:S(2)}, u32[]{:S(2)}) collective-permute-start(bf16[256,2560]{1,0:T(8,128)(2,1)} %slice.64), channel_id=1, source_target_pairs={{0,12},{4,0},{8,4},{12,8},{1,13},{5,1},{9,5},{13,9},{2,14},{6,2},{... | collective-permute-start | bytes 3932168 | tf_op jit(solution)/shard_map/ppermute | solution.py:72
  188.0 3.4 constant_dynamic-update-slice_fusion.3
  191.4 3.4 constant_dynamic-update-slice_fusion.2
  194.8 1.7 broadcast_select_fusion.3
  196.8 12.4 %collective-permute-done.8 = bf16[256,2560]{1,0:T(8,128)(2,1)} collective-permute-done((bf16[256,2560]{1,0:T(8,128)(2,1)}, bf16[256,2560]{1,0:T(8,128)(2,1)}, u32[]{:S(2)}, u32[]{:S(2)}) %collective-permute-start.8) | collective-permute-done | bytes 1310752 | tf_op jit(solution)/shard_map/ppermute | solution.py:71
  209.2 2.5 constant_dynamic-update-slice_fusion.1
  212.6 2.5 constant_dynamic-update-slice_fusion
  215.1 19.2 %fusion = f32[2560,1280]{0,1:T(8,128)} fusion(bf16[2048,2560]{1,0:T(8,128)(2,1)} %constant_dynamic-update-slice_fusion, bf16[2048,320]{0,1:T(8,128)(2,1)S(1)} %get-tuple-element.49, bf16[2048,320]{0,1:T(8,128)(2,1)S(1)} %get-tuple-element.48, bf16[2048,320]{0,1:T(8,128)(2,1)S(1)} %get-tuple-element.47, bf16[2048,320]{0,1:T(8,128)(2,1)S(1)} %get-tuple-element.43), kind=kOutput, calls=%fused_computation.5 | convolution fusion | flops 13442744320 | bytes 28835840 | tf_op jit(solution)/shard_map/dot_general | solution.py:144
  234.3 5.7 %multiply_convert_fusion = (bf16[2560,320]{0,1:T(8,128)(2,1)S(1)}, bf16[2560,320]{0,1:T(8,128)(2,1)S(1)}) fusion(f32[2560,320]{0,1:T(8,128)S(1)} %copy.42, f32[2560,1280]{0,1:T(8,128)} %fusion), kind=kLoop, calls=%fused_computation.23 | loop fusion | flops 9011200 | bytes 19660800 | tf_op jit(solution)/shard_map/convert_element_type | solution.py:154
  240.2 3.4 copy.45
  243.7 49.0 %reduce-scatter.7.cloned.1.call-done = bf16[320,640]{1,0:T(8,128)(2,1)} async-done(((bf16[2560,640]{1,0:T(8,128)(2,1)}), bf16[320,640]{1,0:T(8,128)(2,1)}) %reduce-scatter.7.cloned.1.call-update) | async-done | bytes 409616
  292.8 45.0 %reduce-scatter.9.cloned.1.call-done = bf16[80,640]{1,0:T(8,128)(2,1)} async-done(((bf16[320,640]{1,0:T(8,128)(2,1)}), bf16[80,640]{1,0:T(8,128)(2,1)}) %reduce-scatter.9.cloned.1.call-update) | async-done | bytes 102416
  339.0 16.4 %all_gather.6 = bf16[320,320]{1,0:T(8,128)(2,1)} all-gather(bf16[80,320]{1,0:T(8,128)(2,1)S(1)} %copy.44), channel_id=1, replica_groups=mesh['zh'=4,'y'=4,'c'=2,'x'=4,'zl'=4] {'zh'}, dimensions={0}, use_global_device_ids=true | all-gather | bytes 256000 | tf_op jit(solution)/shard_map/all_gather | solution.py:123
  355.5 10.5 %gather_fusion = bf16[512,2560]{1,0:T(8,128)(2,1)S(1)} fusion(bf16[2048,2560]{1,0:T(8,128)(2,1)} %constant_dynamic-update-slice_fusion, s32[1024]{0:T(1024)S(1)} %pad_clamp_fusion), kind=kCustom, calls=%fused_computation | custom fusion | bytes 5244928 | tf_op jit(solution)/shard_map/jit(_take)/gather | solution.py:160
  366.0 23.3 %all-gather.2.cloned.1.call-done = bf16[2560,320]{1,0:T(8,128)(2,1)} async-done(((bf16[320,320]{1,0:T(8,128)(2,1)}), bf16[2560,320]{1,0:T(8,128)(2,1)}) %all-gather.2.cloned.1.call-update) | async-done | bytes 1638416 | tf_op jit(solution)/shard_map/all_gather | solution.py:123
  389.3 3.4 fusion.20
  (88 shorter events, 14.2 us)
Async XLA Ops:
  7.2 8.4 %copy-start.3 = (s32[128]{0:T(128)S(1)}, s32[128]{0:T(128)}, u32[]{:S(2)}) copy-start(s32[128]{0:T(128)} %param.10) | copy-start | bytes 1540
  7.2 13.7 %copy-start = (bf16[128,5120]{1,0:T(8,128)(2,1)S(1)}, bf16[128,5120]{1,0:T(8,128)(2,1)}, u32[]{:S(2)}) copy-start(bf16[128,5120]{1,0:T(8,128)(2,1)} %param.8) | copy-start | bytes 3932164
  9.0 25.2 %collective-permute-start = (bf16[128,2560]{1,0:T(8,128)(2,1)S(1)}, bf16[128,2560]{1,0:T(8,128)(2,1)}, u32[]{:S(2)}, u32[]{:S(2)}) collective-permute-start(bf16[128,2560]{1,0:T(8,128)(2,1)S(1)} %copy.35), channel_id=1, source_target_pairs={{0,1},{1,2},{2,3},{4,5},{5,6},{6,7},{8,9},{9,10},{10,11},{12,13},{... | collective-permute-start | bytes 1966088 | tf_op jit(solution)/shard_map/ppermute | solution.py:50
  14.2 20.7 %collective-permute-start.1 = (bf16[128,2560]{1,0:T(8,128)(2,1)S(1)}, bf16[128,2560]{1,0:T(8,128)(2,1)S(1)}, u32[]{:S(2)}, u32[]{:S(2)}) collective-permute-start(bf16[128,2560]{1,0:T(8,128)(2,1)S(1)} %copy.35), channel_id=1, source_target_pairs={{1,0},{2,1},{3,2},{5,4},{6,5},{7,6},{9,8},{10,9},{11,10},{13,12},{... | collective-permute-start | bytes 1966088 | tf_op jit(solution)/shard_map/ppermute | solution.py:51
  15.5 93.0 %collective-permute-start.10 = (s32[128]{0:T(128)S(1)}, s32[128]{0:T(128)S(1)}, u32[]{:S(2)}, u32[]{:S(2)}) collective-permute-start(s32[128]{0:T(128)S(1)} %copy-done.3), channel_id=1, source_target_pairs={{0,1},{1,2},{2,3},{4,5},{5,6},{6,7},{8,9},{9,10},{10,11},{12,13},{... | collective-permute-start | bytes 1544 | tf_op jit(solution)/shard_map/ppermute | solution.py:50
  19.5 89.7 %collective-permute-start.11 = (s32[128]{0:T(128)S(1)}, s32[128]{0:T(128)S(1)}, u32[]{:S(2)}, u32[]{:S(2)}) collective-permute-start(s32[128]{0:T(128)S(1)} %copy-done.3), channel_id=1, source_target_pairs={{1,0},{2,1},{3,2},{5,4},{6,5},{7,6},{9,8},{10,9},{11,10},{13,12},{... | collective-permute-start | bytes 1544 | tf_op jit(solution)/shard_map/ppermute | solution.py:51
  22.3 172.5 %all-to-all-start = ((bf16[128,16,320]{0,2,1:T(8,128)(2,1)}), bf16[128,16,320]{0,2,1:T(8,128)(2,1)}, u32[]{:S(2)}, u32[]{:S(2)}) async-start(bf16[128,16,320]{0,2,1:T(8,128)(2,1)} %bitcast.6), calls=%async_computation | async-start | bytes 2621440 | tf_op jit(solution)/shard_map/all_to_all | solution.py:129
  30.2 262.5 %reduce-scatter.7.cloned.1.call-start = ((), (), s32[]{:S(2)}) async-start(), calls=%async_computation.4 | async-start | bytes 3686400
  34.2 3.2 collective-permute-start.2
  34.9 31.9 %collective-permute-start.3 = (bf16[128,2560]{1,0:T(8,128)(2,1)S(1)}, bf16[128,2560]{1,0:T(8,128)(2,1)S(1)}, u32[]{:S(2)}, u32[]{:S(2)}) collective-permute-start(bf16[128,2560]{1,0:T(8,128)(2,1)S(1)} %collective-permute-done.1), channel_id=1, source_target_pairs={{1,0},{2,1},{5,4},{6,5},{9,8},{10,9},{13,12},{14,13},{17,16},{18,1... | collective-permute-start | bytes 1966088 | tf_op jit(solution)/shard_map/ppermute | solution.py:51
  37.5 30.8 %collective-permute-start.4 = (bf16[128,2560]{1,0:T(8,128)(2,1)S(1)}, bf16[128,2560]{1,0:T(8,128)(2,1)S(1)}, u32[]{:S(2)}, u32[]{:S(2)}) collective-permute-start(bf16[128,2560]{1,0:T(8,128)(2,1)S(1)} %collective-permute-done.2), channel_id=1, source_target_pairs={{2,3},{6,7},{10,11},{14,15},{18,19},{22,23},{26,27},{30,31},{34,35... | collective-permute-start | bytes 1966088 | tf_op jit(solution)/shard_map/ppermute | solution.py:50
  66.9 23.8 %collective-permute-start.5 = (bf16[128,2560]{1,0:T(8,128)(2,1)S(1)}, bf16[128,2560]{1,0:T(8,128)(2,1)S(1)}, u32[]{:S(2)}, u32[]{:S(2)}) collective-permute-start(bf16[128,2560]{1,0:T(8,128)(2,1)S(1)} %collective-permute-done.3), channel_id=1, source_target_pairs={{1,0},{5,4},{9,8},{13,12},{17,16},{21,20},{25,24},{29,28},{33,32},... | collective-permute-start | bytes 1966088 | tf_op jit(solution)/shard_map/ppermute | solution.py:51
  95.4 9.2 %copy-start.2 = (s32[1,2048]{1,0:T(1,128)S(1)}, s32[1,2048]{1,0:T(1,128)}, u32[]{:S(2)}) copy-start(s32[1,2048]{1,0:T(1,128)} %param.11) | copy-start | bytes 24580
  98.0 78.3 %collective-permute-start.6 = (bf16[512,2560]{1,0:T(8,128)(2,1)}, bf16[512,2560]{1,0:T(8,128)(2,1)}, u32[]{:S(2)}, u32[]{:S(2)}) collective-permute-start(bf16[512,2560]{1,0:T(8,128)(2,1)} %get-tuple-element.45), channel_id=1, source_target_pairs={{0,4},{4,8},{8,12},{12,0},{1,5},{5,9},{9,13},{13,1},{2,6},{6,10},{... | collective-permute-start | bytes 7864328 | tf_op jit(solution)/shard_map/ppermute | solution.py:69
  100.4 80.3 %collective-permute-start.7 = (bf16[512,2560]{1,0:T(8,128)(2,1)}, bf16[512,2560]{1,0:T(8,128)(2,1)}, u32[]{:S(2)}, u32[]{:S(2)}) collective-permute-start(bf16[512,2560]{1,0:T(8,128)(2,1)} %get-tuple-element.45), channel_id=1, source_target_pairs={{0,12},{4,0},{8,4},{12,8},{1,13},{5,1},{9,5},{13,9},{2,14},{6,2},{... | collective-permute-start | bytes 7864328 | tf_op jit(solution)/shard_map/ppermute | solution.py:70
  108.5 2.0 collective-permute-start.12
  109.2 5.9 %collective-permute-start.13 = (s32[128]{0:T(128)S(1)}, s32[128]{0:T(128)S(1)}, u32[]{:S(2)}, u32[]{:S(2)}) collective-permute-start(s32[128]{0:T(128)S(1)} %collective-permute-done.11), channel_id=1, source_target_pairs={{1,0},{2,1},{5,4},{6,5},{9,8},{10,9},{13,12},{14,13},{17,16},{18,1... | collective-permute-start | bytes 1544 | tf_op jit(solution)/shard_map/ppermute | solution.py:51
  110.5 7.0 %collective-permute-start.14 = (s32[128]{0:T(128)S(1)}, s32[128]{0:T(128)S(1)}, u32[]{:S(2)}, u32[]{:S(2)}) collective-permute-start(s32[128]{0:T(128)S(1)} %collective-permute-done.12), channel_id=1, source_target_pairs={{2,3},{6,7},{10,11},{14,15},{18,19},{22,23},{26,27},{30,31},{34,35... | collective-permute-start | bytes 1544 | tf_op jit(solution)/shard_map/ppermute | solution.py:50
  115.2 4.7 %collective-permute-start.15 = (s32[128]{0:T(128)S(1)}, s32[128]{0:T(128)S(1)}, u32[]{:S(2)}, u32[]{:S(2)}) collective-permute-start(s32[128]{0:T(128)S(1)} %collective-permute-done.13), channel_id=1, source_target_pairs={{1,0},{5,4},{9,8},{13,12},{17,16},{21,20},{25,24},{29,28},{33,32},... | collective-permute-start | bytes 1544 | tf_op jit(solution)/shard_map/ppermute | solution.py:51
  120.1 37.9 %collective-permute-start.16 = (s32[512]{0:T(512)S(1)}, s32[512]{0:T(512)S(1)}, u32[]{:S(2)}, u32[]{:S(2)}) collective-permute-start(s32[512]{0:T(512)S(1)} %get-tuple-element.54), channel_id=1, source_target_pairs={{0,4},{4,8},{8,12},{12,0},{1,5},{5,9},{9,13},{13,1},{2,6},{6,10},{... | collective-permute-start | bytes 6152 | tf_op jit(solution)/shard_map/ppermute | solution.py:69
  122.0 38.1 %collective-permute-start.17 = (s32[512]{0:T(512)S(1)}, s32[512]{0:T(512)S(1)}, u32[]{:S(2)}, u32[]{:S(2)}) collective-permute-start(s32[512]{0:T(512)S(1)} %get-tuple-element.54), channel_id=1, source_target_pairs={{0,12},{4,0},{8,4},{12,8},{1,13},{5,1},{9,5},{13,9},{2,14},{6,2},{... | collective-permute-start | bytes 6152 | tf_op jit(solution)/shard_map/ppermute | solution.py:70
  158.0 15.1 %collective-permute-start.18 = (s32[256]{0:T(256)S(1)}, s32[256]{0:T(256)S(1)}, u32[]{:S(2)}, u32[]{:S(2)}) collective-permute-start(s32[256]{0:T(256)S(1)} %slice.49), channel_id=1, source_target_pairs={{0,4},{4,8},{8,12},{12,0},{1,5},{5,9},{9,13},{13,1},{2,6},{6,10},{... | collective-permute-start | bytes 3080 | tf_op jit(solution)/shard_map/ppermute | solution.py:71
  160.2 13.2 %collective-permute-start.19 = (s32[256]{0:T(256)S(1)}, s32[256]{0:T(256)S(1)}, u32[]{:S(2)}, u32[]{:S(2)}) collective-permute-start(s32[256]{0:T(256)S(1)} %slice.50), channel_id=1, source_target_pairs={{0,12},{4,0},{8,4},{12,8},{1,13},{5,1},{9,5},{13,9},{2,14},{6,2},{... | collective-permute-start | bytes 3080 | tf_op jit(solution)/shard_map/ppermute | solution.py:72
  178.7 30.4 %collective-permute-start.8 = (bf16[256,2560]{1,0:T(8,128)(2,1)}, bf16[256,2560]{1,0:T(8,128)(2,1)}, u32[]{:S(2)}, u32[]{:S(2)}) collective-permute-start(bf16[256,2560]{1,0:T(8,128)(2,1)} %slice.63), channel_id=1, source_target_pairs={{0,4},{4,8},{8,12},{12,0},{1,5},{5,9},{9,13},{13,1},{2,6},{6,10},{... | collective-permute-start | bytes 3932168 | tf_op jit(solution)/shard_map/ppermute | solution.py:71
  183.2 29.4 %collective-permute-start.9 = (bf16[256,2560]{1,0:T(8,128)(2,1)}, bf16[256,2560]{1,0:T(8,128)(2,1)}, u32[]{:S(2)}, u32[]{:S(2)}) collective-permute-start(bf16[256,2560]{1,0:T(8,128)(2,1)} %slice.64), channel_id=1, source_target_pairs={{0,12},{4,0},{8,4},{12,8},{1,13},{5,1},{9,5},{13,9},{2,14},{6,2},{... | collective-permute-start | bytes 3932168 | tf_op jit(solution)/shard_map/ppermute | solution.py:72
  243.6 94.1 %reduce-scatter.9.cloned.1.call-start = ((), (), s32[]{:S(2)}) async-start(), calls=%async_computation.5 | async-start | bytes 512000
  292.7 96.6 %all-gather.2.cloned.1.call-start = ((), (), s32[]{:S(2)}) async-start(), calls=%async_computation.3 | async-start | bytes 2211840 | tf_op jit(solution)/shard_map/all_gather | solution.py:123
  339.0 27.0 %copy-start.1 = (bf16[80,320]{1,0:T(8,128)(2,1)}, bf16[80,320]{1,0:T(8,128)(2,1)S(1)}, u32[]{:S(2)}) copy-start(bf16[80,320]{1,0:T(8,128)(2,1)S(1)} %copy.44) | copy-start | bytes 153604
Sparse Core Ops, SparseCore 0:
  243.8 48.8 reduce-scatter.6
  295.8 41.9 reduce-scatter.8
  355.5 33.7 all-gather.1

commit v4 on v2

--- a/solution.py
+++ b/solution.py
@@ -17,6 +17,7 @@
 SITE_SUB = (("zh", 4), ("y", 4), ("c", 2))
 SHARD_SUB = (("x", 4), ("zl", 4))
 SCATTER_STAGES = (("y", "c"), ("zh",))
+FEATURE_PIECES = 2
 
 
 def count_same(site_ids):
@@ -49,10 +50,15 @@
         )
         return jnp.transpose(x, order).reshape(shape)
 
-    def gather_events(x):
-        for name in reversed(shard_names):
+    def gather_events(x, pieces):
+        names = tuple(reversed(shard_names))
+        for name in names[:-1]:
             x = lax.all_gather(x, name, axis=0, tiled=True)
-        return x
+        width = x.shape[1] // pieces
+        return [
+            lax.all_gather(x[:, k * width : (k + 1) * width], names[-1], axis=0, tiled=True)
+            for k in range(pieces)
+        ]
 
     def scatter_sites(x):
         for stage in scatter_stages:
@@ -67,10 +73,10 @@
     def on_device(activations, out_grads, theta, token_ids, assignment):
         head_cols = HEADS * HEAD_DIM
         site_ids = lax.all_gather(token_ids, shard_names, axis=0, tiled=True)
-        site_acts = gather_events(to_position_order(activations, 1))
+        acts_pieces = gather_events(to_position_order(activations, 1), FEATURE_PIECES)
         grad_cols = lax.all_to_all(out_grads, shard_names, split_axis=1, concat_axis=0, tiled=True)
         theta_rows = to_position_order(theta[0], 0)
-        site_events = site_acts.shape[0]
+        site_events = acts_pieces[0].shape[0]
         micro_rows = site_events // MICRO
         ordering = assignment[0]
         counts = count_same(site_ids)
@@ -83,23 +89,33 @@
             [jnp.where((batch_of == m)[:, None], scaled, jnp.zeros_like(scaled)) for m in range(MICRO)],
             axis=1,
         )
-        gradients = lax.dot_general(
-            site_acts, masked, (((0,), (0,)), ((), ())), preferred_element_type=jnp.float32
-        )
         cols = scaled.shape[1]
-        fisher = gradients[:, :cols] * gradients[:, :cols]
-        for micro in range(1, MICRO):
-            g = gradients[:, micro * cols : (micro + 1) * cols]
-            fisher = fisher + g * g
-        fisher = fisher / MICRO
-        product = fisher * theta_rows.astype(jnp.float32)
-        both = jnp.concatenate([product.astype(jnp.bfloat16), fisher.astype(jnp.bfloat16)], axis=1)
+        blocks = []
+        row_start = 0
+        for piece in acts_pieces:
+            gradients = lax.dot_general(
+                piece, masked, (((0,), (0,)), ((), ())), preferred_element_type=jnp.float32
+            )
+            fisher = gradients[:, :cols] * gradients[:, :cols]
+            for micro in range(1, MICRO):
+                g = gradients[:, micro * cols : (micro + 1) * cols]
+                fisher = fisher + g * g
+            fisher = fisher / MICRO
+            rows = piece.shape[1]
+            product = fisher * theta_rows[row_start : row_start + rows].astype(jnp.float32)
+            row_start += rows
+            blocks.append(
+                jnp.concatenate([product.astype(jnp.bfloat16), fisher.astype(jnp.bfloat16)], axis=1)
+            )
+        both = jnp.concatenate(blocks, axis=0)
         summed = scatter_sites(both).astype(jnp.float32)
         numerator, denominator = summed[:, :cols], summed[:, cols:]
         owned = (numerator / (denominator + epsilon)).astype(jnp.bfloat16)
         whole_merged = gather_sites(owned)
         scaling = float(head_cols) ** (-0.5)
-        probe = jnp.take(site_acts, ordering[:micro_rows], axis=0)
+        probe = jnp.concatenate(
+            [jnp.take(piece, ordering[:micro_rows], axis=0) for piece in acts_pieces], axis=1
+        )
         response = (
             jnp.dot(probe, whole_merged, preferred_element_type=jnp.float32) * scaling
         ).astype(jnp.bfloat16)

time: 373 us -> 402 us (1.078)
  waiting for transfers between devices: 211 us -> 226 us
  other arithmetic: 15.9 us -> 26.2 us
  blocking collectives: 71.2 us -> 62.9 us
  local copies, waits for them, and re-layouts: 29.4 us -> 36.3 us
  matrix products: 24.2 us -> 28.8 us
    all_gather x0 -> x2, waiting for transfers between devices: none -> 50.1 us  [gather_events(): lax.all_gather(x[:, k * width:(k + 1) * width], names[-1], axis=0, tiled=...]
    all_gather x2 -> x1, waiting for transfers between devices: 99.7 us -> 69.1 us  [gather_events(): x = lax.all_gather(x, name, axis=0, tiled=True)]
    concatenate x1, other arithmetic: 0.21 us -> 13.5 us  [on_device(): both = jnp.concatenate(blocks, axis=0)]
    all_gather x1, blocking collectives: 54.1 us -> 46.4 us  [on_device(): site_ids = lax.all_gather(token_ids, shard_names, axis=0, tiled=True)]
    dot_general x1 -> x2, matrix products: 20.7 us -> 24.6 us  [on_device(): lax.dot_general(piece, masked, (((0,), (0,)), ((), ())), preferred_elemen...]
    unnamed x15 -> x25, local copies, waits for them, and re-layouts: 11.1 us -> 13.1 us
    gather x1 -> x2, local copies, waits for them, and re-layouts: 10.5 us -> 12.6 us  [on_device(): jnp.take(piece, ordering[:micro_rows], axis=0)]
    unnamed x7 -> x8, waiting for transfers between devices: 89.6 us -> 87.7 us
  transfers between devices with their start and end apart: 6 -> 7, of which waited for: 5 -> 5; matrix products, arithmetic and copies ran while one was open for 9% -> 12% of each run, Pallas kernels for 0% -> 0%
where the time goes in v4:
time: 402 us; the launch traced here: 401 us
  waiting for transfers between devices  226 us (56%)
  blocking collectives  62.9 us (16%)
  local copies, waits for them, and re-layouts  36.3 us (9%)
  matrix products  28.8 us (7%)
  other arithmetic  26.2 us (7%)
  between operations  14.4 us (4%)
  starting transfers between devices  6.31 us (2%)
    unnamed x8, waiting for transfers between devices  87.7 us
    all_gather x1, waiting for transfers between devices, gather_events(): x = lax.all_gather(x, name, axis=0, tiled=True)  69.1 us
    all_gather x2, waiting for transfers between devices, gather_events(): lax.all_gather(x[:, k * width:(k + 1) * width], names[-1], axis=0, tiled=...  50.1 us
    all_gather x1, blocking collectives, on_device(): site_ids = lax.all_gather(token_ids, shard_names, axis=0, tiled=True)  46.4 us
    dot_general x2, matrix products, on_device(): lax.dot_general(piece, masked, (((0,), (0,)), ((), ())), preferred_elemen...  24.6 us
    all_gather x1, waiting for transfers between devices, gather_sites(): x = lax.all_gather(x, stage, axis=0, tiled=True)  19.5 us
    all_gather x1, blocking collectives, gather_sites(): x = lax.all_gather(x, stage, axis=0, tiled=True)  16.6 us
    concatenate x1, other arithmetic, on_device(): both = jnp.concatenate(blocks, axis=0)  13.5 us
  transfers between devices with their start and end apart: 7, of which 5 were waited for; matrix products, arithmetic and copies ran while one was open for 12% of the time, Pallas kernels for 0%

profile of v4, /device:TPU:1, one launch (start us, length us, event | category | flops | bytes accessed | tf_op | source)
XLA Modules:
  0.0 401.4 jit_solution(5155019455039912309)
XLA Ops:
  7.2 1.4 copy.35
  8.7 1.1 copy.37
  9.8 0.0 all-gather.10.cloned.1.call-start
  9.8 69.1 %all-gather.6.cloned.1.call-done = bf16[512,2560]{1,0:T(8,128)(2,1)} async-done(((bf16[128,2560]{1,0:T(8,128)(2,1)}), bf16[512,2560]{1,0:T(8,128)(2,1)}) %all-gather.6.cloned.1.call-update) | async-done | bytes 2621456 | tf_op jit(solution)/shard_map/all_gather | solution.py:56
  78.9 3.5 fusion.30
  82.4 1.3 copy-done.4
  83.7 1.4 copy.33
  85.2 5.9 %all-to-all-start = ((bf16[128,16,320]{0,2,1:T(8,128)(2,1)}), bf16[128,16,320]{0,2,1:T(8,128)(2,1)S(1)}, u32[]{:S(2)}, u32[]{:S(2)}) async-start(bf16[128,16,320]{0,2,1:T(8,128)(2,1)} %bitcast.3), calls=%async_computation | async-start | bytes 2621440 | tf_op jit(solution)/shard_map/all_to_all | solution.py:77
  91.0 0.0 all-gather.8.cloned.1.call-start
  91.1 0.7 all-gather.8.cloned.1.call-update
  91.8 3.6 copy.38
  95.4 1.5 slice_convert_fusion.1
  97.0 0.1 copy.41
  97.1 1.7 copy.42
  98.8 46.4 %all-gather = s32[16,1,128]{2,1,0:T(1,128)S(1)} all-gather(s32[1,1,128]{2,1,0:T(1,128)S(1)} %bitcast.52), channel_id=1, replica_groups=mesh['zh'=4,'y'=4,'c'=2,'x'=4,'zl'=4] {'x','zl'}, dimensions={0}, use_global_device_ids=true | all-gather | bytes 8704 | tf_op jit(solution)/shard_map/all_gather | solution.py:75
  145.2 0.5 broadcast.84
  145.7 0.7 reduce.3
  146.4 2.7 while.10
  146.5 0.6 convert_reduce_fusion.2
  147.1 0.6 convert_reduce_fusion.2
  147.8 0.6 convert_reduce_fusion.2
  148.5 0.6 convert_reduce_fusion.2
  149.2 1.7 copy.39
  150.9 1.7 copy.40
  152.6 1.7 select_reduce_fusion
  154.4 0.4 broadcast_select_fusion.5
  154.7 1.8 broadcast_select_fusion.4
  156.5 12.5 %convolution_bitcast_fusion = f32[1280,1280]{0,1:T(8,128)S(1)} fusion(bf16[2048,1280]{1,0:T(8,128)(2,1)} %all-gather.10.cloned.1.call-done, bf16[2048,320]{0,1:T(8,128)(2,1)} %get-tuple-element.54, bf16[2048,320]{0,1:T(8,128)(2,1)} %get-tuple-element.53, bf16[2048,320]{0,1:T(8,128)(2,1)S(1)} %get-tuple-element.52, bf16[2048,320]{0,1:T(8,128)(2,1)S(1)} %get-tuple-element.46), kind=kOutput, calls=%fused_computation.6 | convolution fusion | flops 6731857920 | bytes 17039360 | tf_op jit(solution)/shard_map/dot_general | solution.py:96
  169.0 1.7 multiply_convert_fusion
  170.8 50.1 %all-gather.8.cloned.1.call-done = bf16[2048,1280]{1,0:T(8,128)(2,1)} async-done(((bf16[512,1280]{1,0:T(8,128)(2,1)}), bf16[2048,1280]{1,0:T(8,128)(2,1)}) %all-gather.8.cloned.1.call-update) | async-done | bytes 5242896 | tf_op jit(solution)/shard_map/all_gather | solution.py:59
  220.8 12.1 %convolution_bitcast_fusion.1 = f32[1280,1280]{0,1:T(8,128)S(1)} fusion(bf16[2048,1280]{1,0:T(8,128)(2,1)} %all-gather.8.cloned.1.call-done, bf16[2048,320]{0,1:T(8,128)(2,1)} %get-tuple-element.54, bf16[2048,320]{0,1:T(8,128)(2,1)} %get-tuple-element.53, bf16[2048,320]{0,1:T(8,128)(2,1)} %copy-done.5, bf16[2048,320]{0,1:T(8,128)(2,1)S(1)} %get-tuple-element.46), kind=kOutput, calls=%fused_computation.7 | convolution fusion | flops 6731857920 | bytes 17039360 | tf_op jit(solution)/shard_map/dot_general | solution.py:96
  233.0 0.6 multiply_convert_fusion.1
  233.6 0.5 copy-done.2
  234.1 0.2 copy-done.3
  234.4 13.5 %maximum_maximum_fusion = bf16[2560,640]{0,1:T(8,128)(2,1)S(1)} fusion(bf16[1280,320]{0,1:T(8,128)(2,1)S(1)} %copy-done.3, bf16[1280,320]{0,1:T(8,128)(2,1)S(1)} %copy-done.2, bf16[1280,320]{0,1:T(8,128)(2,1)S(1)} %get-tuple-element.43, bf16[1280,320]{0,1:T(8,128)(2,1)S(1)} %get-tuple-element.42), kind=kLoop, calls=%fused_computation.9 | loop fusion | flops 13107200 | bytes 6553600 | tf_op jit(solution)/shard_map/concatenate | solution.py:110
  247.9 3.4 copy.45
  251.4 0.3 reduce-scatter.9.cloned.1.call-start
  251.6 42.2 %reduce-scatter.7.cloned.1.call-done = bf16[320,640]{1,0:T(8,128)(2,1)} async-done(((bf16[2560,640]{1,0:T(8,128)(2,1)}), bf16[320,640]{1,0:T(8,128)(2,1)}) %reduce-scatter.7.cloned.1.call-update) | async-done | bytes 409616
  293.8 0.0 all-gather.12.cloned.1.call-start
  293.9 44.8 %reduce-scatter.9.cloned.1.call-done = bf16[80,640]{1,0:T(8,128)(2,1)} async-done(((bf16[320,640]{1,0:T(8,128)(2,1)}), bf16[80,640]{1,0:T(8,128)(2,1)}) %reduce-scatter.9.cloned.1.call-update) | async-done | bytes 102416
  338.7 1.1 copy.48
  339.8 0.1 copy.44
  339.9 16.6 %all_gather.22 = bf16[320,320]{1,0:T(8,128)(2,1)} all-gather(bf16[80,320]{1,0:T(8,128)(2,1)S(1)} %copy.44), channel_id=1, replica_groups=mesh['zh'=4,'y'=4,'c'=2,'x'=4,'zl'=4] {'zh'}, dimensions={0}, use_global_device_ids=true | all-gather | bytes 256000 | tf_op jit(solution)/shard_map/all_gather | solution.py:70
  356.5 6.3 %gather_fusion = bf16[512,1280]{1,0:T(8,128)(2,1)S(1)} fusion(bf16[2048,1280]{1,0:T(8,128)(2,1)} %all-gather.8.cloned.1.call-done, s32[1024]{0:T(1024)S(1)} %pad_clamp_fusion), kind=kCustom, calls=%fused_computation.clone | custom fusion | bytes 2623488 | tf_op jit(solution)/shard_map/jit(_take)/gather | solution.py:117
  362.8 6.3 %gather_fusion.1 = bf16[512,1280]{1,0:T(8,128)(2,1)S(1)} fusion(bf16[2048,1280]{1,0:T(8,128)(2,1)} %all-gather.10.cloned.1.call-done, s32[1024]{0:T(1024)S(1)} %pad_clamp_fusion), kind=kCustom, calls=%fused_computation.1.clone | custom fusion | bytes 2623488 | tf_op jit(solution)/shard_map/jit(_take)/gather | solution.py:117
  369.1 1.8 broadcast_select_fusion.1
  370.9 19.5 %all-gather.12.cloned.1.call-done = bf16[2560,320]{1,0:T(8,128)(2,1)} async-done(((bf16[320,320]{1,0:T(8,128)(2,1)}), bf16[2560,320]{1,0:T(8,128)(2,1)}) %all-gather.12.cloned.1.call-update) | async-done | bytes 1638416 | tf_op jit(solution)/shard_map/all_gather | solution.py:70
  390.4 4.2 %fusion.16 = bf16[512,320]{0,1:T(8,128)(2,1)} fusion(bf16[2560,320]{1,0:T(8,128)(2,1)} %all-gather.12.cloned.1.call-done, bf16[512,1280]{1,0:T(8,128)(2,1)} %get-tuple-element.60, bf16[512,1280]{1,0:T(8,128)(2,1)} %get-tuple-element.59), kind=kOutput, calls=%fused_computation.42 | convolution fusion | flops 844431360 | bytes 4587520 | tf_op jit(solution)/shard_map/dot_general | solution.py:120
  (45 shorter events, 0.6 us)
Async XLA Ops:
  7.2 71.8 %all-gather.6.cloned.1.call-start = ((), (), s32[]{:S(2)}) async-start(), calls=%async_computation.3 | async-start | bytes 3276800 | tf_op jit(solution)/shard_map/all_gather | solution.py:56
  9.8 146.7 %all-gather.10.cloned.1.call-start = ((), (), s32[]{:S(2)}) async-start(), calls=%async_computation.5 | async-start | bytes 6553600 | tf_op jit(solution)/shard_map/all_gather | solution.py:59
  82.4 1.3 copy-start.4
  85.2 69.2 %all-to-all-start = ((bf16[128,16,320]{0,2,1:T(8,128)(2,1)}), bf16[128,16,320]{0,2,1:T(8,128)(2,1)S(1)}, u32[]{:S(2)}, u32[]{:S(2)}) async-start(bf16[128,16,320]{0,2,1:T(8,128)(2,1)} %bitcast.3), calls=%async_computation | async-start | bytes 2621440 | tf_op jit(solution)/shard_map/all_to_all | solution.py:77
  91.0 129.8 %all-gather.8.cloned.1.call-start = ((), (), s32[]{:S(2)}) async-start(), calls=%async_computation.4 | async-start | bytes 6553600 | tf_op jit(solution)/shard_map/all_gather | solution.py:59
  91.8 202.0 %reduce-scatter.7.cloned.1.call-start = ((), (), s32[]{:S(2)}) async-start(), calls=%async_computation.7 | async-start | bytes 3686400
  97.1 1.7 copy-start.7
  150.9 1.7 copy-start.8
  156.5 12.5 %copy-start.5 = (bf16[2048,320]{0,1:T(8,128)(2,1)}, bf16[2048,320]{0,1:T(8,128)(2,1)S(1)}, u32[]{:S(2)}) copy-start(bf16[2048,320]{0,1:T(8,128)(2,1)S(1)} %get-tuple-element.52) | copy-start | bytes 3932164
  156.5 12.5 %copy-start = (f32[1280,320]{0,1:T(8,128)S(1)}, f32[1280,320]{0,1:T(8,128)}, u32[]{:S(2)}) copy-start(f32[1280,320]{0,1:T(8,128)} %copy.42) | copy-start | bytes 4915204
  170.8 62.2 %copy-start.1 = (f32[1280,320]{0,1:T(8,128)S(1)}, f32[1280,320]{0,1:T(8,128)}, u32[]{:S(2)}) copy-start(f32[1280,320]{0,1:T(8,128)} %copy.40) | copy-start | bytes 4915204
  233.0 1.1 copy-start.2
  233.0 1.4 copy-start.3
  251.4 87.3 %reduce-scatter.9.cloned.1.call-start = ((), (), s32[]{:S(2)}) async-start(), calls=%async_computation.8 | async-start | bytes 512000
  293.8 96.5 %all-gather.12.cloned.1.call-start = ((), (), s32[]{:S(2)}) async-start(), calls=%async_computation.6 | async-start | bytes 2211840 | tf_op jit(solution)/shard_map/all_gather | solution.py:70
  339.9 22.9 %copy-start.6 = (bf16[80,320]{1,0:T(8,128)(2,1)}, bf16[80,320]{1,0:T(8,128)(2,1)S(1)}, u32[]{:S(2)}) copy-start(bf16[80,320]{1,0:T(8,128)(2,1)S(1)} %copy.44) | copy-start | bytes 153604
Sparse Core Ops, SparseCore 0:
  10.1 68.7 all-gather.5
  82.5 69.7 all-gather.9
  154.5 66.3 all-gather.7
  251.5 42.2 reduce-scatter.6
  296.7 41.8 reduce-scatter.8
  356.6 33.7 all-gather.11

commit v5 on v2

--- a/solution.py
+++ b/solution.py
@@ -49,8 +49,16 @@
         )
         return jnp.transpose(x, order).reshape(shape)
 
+    def all_to_all_gather(x, names):
+        group = math.prod(size for name, size in shard_axes if name in names)
+        copies = jnp.broadcast_to(x[None], (group,) + x.shape)
+        gathered = lax.all_to_all(copies, names, 0, 0, tiled=True)
+        return gathered.reshape((group * x.shape[0],) + x.shape[1:])
+
     def gather_events(x):
-        for name in reversed(shard_names):
+        names = tuple(reversed(shard_names))
+        x = all_to_all_gather(x, names[0])
+        for name in names[1:]:
             x = lax.all_gather(x, name, axis=0, tiled=True)
         return x
 
@@ -66,7 +74,7 @@
 
     def on_device(activations, out_grads, theta, token_ids, assignment):
         head_cols = HEADS * HEAD_DIM
-        site_ids = lax.all_gather(token_ids, shard_names, axis=0, tiled=True)
+        site_ids = all_to_all_gather(token_ids, shard_names)
         site_acts = gather_events(to_position_order(activations, 1))
         grad_cols = lax.all_to_all(out_grads, shard_names, split_axis=1, concat_axis=0, tiled=True)
         theta_rows = to_position_order(theta[0], 0)

time: 373 us -> 374 us (level)
  waiting for transfers between devices: 211 us -> 197 us
  blocking collectives: 71.2 us -> 80.7 us
  starting transfers between devices: 6.1 us -> 11.2 us
    all_to_all x0 -> x1, blocking collectives: none -> 64.3 us  [all_to_all_gather(): gathered = lax.all_to_all(copies, names, 0, 0, tiled=True)]
    all_gather x1 -> x0, blocking collectives: 54.1 us -> none  [on_device(): site_ids = lax.all_gather(token_ids, shard_names, axis=0, tiled=True)]
    all_gather x2 -> x1, waiting for transfers between devices: 99.7 us -> 65.4 us  [gather_events(): x = lax.all_gather(x, name, axis=0, tiled=True)]
    all_to_all x1, waiting for transfers between devices: 0.01 us -> 16.6 us  [on_device(): lax.all_to_all(out_grads, shard_names, split_axis=1, concat_axis=0, tiled...]
    all_to_all x0 -> x1, starting transfers between devices: none -> 6.63 us  [all_to_all_gather(): gathered = lax.all_to_all(copies, names, 0, 0, tiled=True)]
    all_to_all x0 -> x1, waiting for transfers between devices: none -> 5.14 us  [all_to_all_gather(): gathered = lax.all_to_all(copies, names, 0, 0, tiled=True)]
    unnamed x7 -> x6, waiting for transfers between devices: 89.6 us -> 87.4 us
  transfers between devices with their start and end apart: 6 -> 6, of which waited for: 5 -> 6; matrix products, arithmetic and copies ran while one was open for 9% -> 9% of each run, Pallas kernels for 0% -> 0%
where the time goes in v5:
time: 374 us; the launch traced here: 373 us
  waiting for transfers between devices  197 us (53%)
  blocking collectives  80.7 us (22%)
  local copies, waits for them, and re-layouts  29.8 us (8%)
  matrix products  24.2 us (6%)
  other arithmetic  15.9 us (4%)
  between operations  14 us (4%)
  starting transfers between devices  11.2 us (3%)
    unnamed x6, waiting for transfers between devices  87.4 us
    all_gather x1, waiting for transfers between devices, gather_events(): x = lax.all_gather(x, name, axis=0, tiled=True)  65.4 us
    all_to_all x1, blocking collectives, all_to_all_gather(): gathered = lax.all_to_all(copies, names, 0, 0, tiled=True)  64.3 us
    all_gather x1, waiting for transfers between devices, gather_sites(): x = lax.all_gather(x, stage, axis=0, tiled=True)  22.7 us
    dot_general x1, matrix products, on_device(): lax.dot_general(site_acts, masked, (((0,), (0,)), ((), ())), preferred_el...  20.7 us
    all_to_all x1, waiting for transfers between devices, on_device(): lax.all_to_all(out_grads, shard_names, split_axis=1, concat_axis=0, tiled...  16.6 us
    all_gather x1, blocking collectives, gather_sites(): x = lax.all_gather(x, stage, axis=0, tiled=True)  16.5 us
    unnamed x15, local copies, waits for them, and re-layouts  11.2 us
  transfers between devices with their start and end apart: 6, of which 6 were waited for; matrix products, arithmetic and copies ran while one was open for 9% of the time, Pallas kernels for 0%

profile of v5, /device:TPU:1, one launch (start us, length us, event | category | flops | bytes accessed | tf_op | source)
XLA Modules:
  0.0 373.1 jit_solution(16797322744990692574)
XLA Ops:
  7.2 0.0 all-gather.3.cloned.1.call-start
  7.2 1.4 copy.30
  8.7 0.2 copy.32
  8.9 0.2 broadcast_in_dim.82
  9.1 0.0 copy-start.3
  9.1 0.0 copy-start
  9.2 64.3 %all_to_all.27 = bf16[4,128,2560]{2,1,0:T(8,128)(2,1)} all-to-all(bf16[4,128,2560]{2,1,0:T(8,128)(2,1)S(1)} %broadcast_in_dim.82), channel_id=1, replica_groups=mesh['zh'=4,'y'=4,'c'=2,'x'=4,'zl'=4] {'zl'}, dimensions={0} | all-to-all | bytes 5242880 | tf_op jit(solution)/shard_map/all_to_all | solution.py:55
  73.4 0.0 all-gather.3.cloned.1.call-update
  73.5 0.6 broadcast_in_dim.77
  74.1 6.6 %all-to-all-start.1 = ((s32[16,1,128]{2,1,0:T(1,128)}), s32[16,1,128]{2,1,0:T(1,128)S(1)}, u32[]{:S(2)}, u32[]{:S(2)}) async-start(s32[16,1,128]{2,1,0:T(1,128)} %broadcast_in_dim.77), calls=%async_computation.1 | async-start | bytes 16384 | tf_op jit(solution)/shard_map/all_to_all | solution.py:55
  80.7 1.5 copy.28
  82.2 5.1 %all-to-all-done.1 = s32[16,1,128]{2,1,0:T(1,128)S(1)} async-done(((s32[16,1,128]{2,1,0:T(1,128)}), s32[16,1,128]{2,1,0:T(1,128)S(1)}, u32[]{:S(2)}, u32[]{:S(2)}) %all-to-all-start.1) | async-done | bytes 8224 | tf_op jit(solution)/shard_map/all_to_all | solution.py:55
  87.4 4.4 %all-to-all-start = ((bf16[128,16,320]{0,2,1:T(8,128)(2,1)}), bf16[128,16,320]{0,2,1:T(8,128)(2,1)}, u32[]{:S(2)}, u32[]{:S(2)}) async-start(bf16[128,16,320]{0,2,1:T(8,128)(2,1)} %bitcast.4), calls=%async_computation | async-start | bytes 2621440 | tf_op jit(solution)/shard_map/all_to_all | solution.py:79
  91.8 0.0 reduce-scatter.7.cloned.1.call-start
  91.8 3.7 copy.33
  95.5 0.4 convert_bitcast_fusion
  95.9 2.3 copy.34
  98.2 3.9 %copy.35 = f32[2560,320]{0,1:T(8,128)S(1)} copy(f32[2560,320]{1,0:T(8,128)} %bitcast.44) | data formatting | bytes 6553600 | tf_op jit(solution)/shard_map/convert_element_type | solution.py:103
  102.1 1.7 select_reduce_fusion
  103.9 0.5 broadcast.98
  104.4 0.7 reduce.3
  105.1 2.7 while.10
  105.1 0.6 convert_reduce_fusion.2
  105.8 0.6 convert_reduce_fusion.2
  106.5 0.6 convert_reduce_fusion.2
  107.1 0.6 convert_reduce_fusion.2
  107.8 16.6 %all-to-all-done = bf16[128,16,320]{0,2,1:T(8,128)(2,1)} async-done(((bf16[128,16,320]{0,2,1:T(8,128)(2,1)}), bf16[128,16,320]{0,2,1:T(8,128)(2,1)}, u32[]{:S(2)}, u32[]{:S(2)}) %all-to-all-start) | async-done | bytes 1310752 | tf_op jit(solution)/shard_map/all_to_all | solution.py:79
  124.4 2.8 broadcast_select_fusion.3
  127.1 2.0 broadcast_select_fusion.2
  129.1 65.4 %all-gather.3.cloned.1.call-done = bf16[2048,2560]{1,0:T(8,128)(2,1)} async-done(((bf16[512,2560]{1,0:T(8,128)(2,1)}), bf16[2048,2560]{1,0:T(8,128)(2,1)}) %all-gather.3.cloned.1.call-update) | async-done | bytes 10485776 | tf_op jit(solution)/shard_map/all_gather | solution.py:62
  194.6 20.7 %convolution_bitcast_fusion = f32[2560,1280]{0,1:T(8,128)} fusion(bf16[2048,2560]{1,0:T(8,128)(2,1)} %all-gather.3.cloned.1.call-done, bf16[2048,320]{0,1:T(8,128)(2,1)} %get-tuple-element.47, bf16[2048,320]{0,1:T(8,128)(2,1)} %get-tuple-element.46, bf16[2048,320]{0,1:T(8,128)(2,1)} %get-tuple-element.45, bf16[2048,320]{0,1:T(8,128)(2,1)} %get-tuple-element.43), kind=kOutput, calls=%fused_computation.5 | convolution fusion | flops 13442744320 | bytes 28835840 | tf_op jit(solution)/shard_map/dot_general | solution.py:94
  215.3 5.7 %multiply_convert_fusion = (bf16[2560,320]{0,1:T(8,128)(2,1)S(1)}, bf16[2560,320]{0,1:T(8,128)(2,1)S(1)}) fusion(f32[2560,320]{0,1:T(8,128)S(1)} %copy.35, f32[2560,1280]{0,1:T(8,128)} %convolution_bitcast_fusion), kind=kLoop, calls=%fused_computation.23 | loop fusion | flops 9011200 | bytes 19660800 | tf_op jit(solution)/shard_map/convert_element_type | solution.py:104
  221.0 0.2 pad_maximum_fusion
  221.2 3.4 copy.38
  224.6 0.0 reduce-scatter.7.cloned.1.call-update
  224.7 0.0 reduce-scatter.9.cloned.1.call-start
  224.7 42.2 %reduce-scatter.7.cloned.1.call-done = bf16[320,640]{1,0:T(8,128)(2,1)} async-done(((bf16[2560,640]{1,0:T(8,128)(2,1)}), bf16[320,640]{1,0:T(8,128)(2,1)}) %reduce-scatter.7.cloned.1.call-update) | async-done | bytes 409616
  266.9 0.0 reduce-scatter.9.cloned.1.call-update
  266.9 0.0 all-gather.5.cloned.1.call-start
  267.0 45.1 %reduce-scatter.9.cloned.1.call-done = bf16[80,640]{1,0:T(8,128)(2,1)} async-done(((bf16[320,640]{1,0:T(8,128)(2,1)}), bf16[80,640]{1,0:T(8,128)(2,1)}) %reduce-scatter.9.cloned.1.call-update) | async-done | bytes 102416
  312.1 1.1 copy.41
  313.2 0.1 copy.37
  313.3 0.0 copy-start.1
  313.3 16.5 %all_gather.10 = bf16[320,320]{1,0:T(8,128)(2,1)} all-gather(bf16[80,320]{1,0:T(8,128)(2,1)S(1)} %copy.37), channel_id=1, replica_groups=mesh['zh'=4,'y'=4,'c'=2,'x'=4,'zl'=4] {'zh'}, dimensions={0}, use_global_device_ids=true | all-gather | bytes 256000 | tf_op jit(solution)/shard_map/all_gather | solution.py:72
  329.8 0.0 all-gather.5.cloned.1.call-update
  329.9 10.5 %gather_fusion = bf16[512,2560]{1,0:T(8,128)(2,1)S(1)} fusion(bf16[2048,2560]{1,0:T(8,128)(2,1)} %all-gather.3.cloned.1.call-done, s32[1024]{0:T(1024)S(1)} %pad_clamp_fusion), kind=kCustom, calls=%fused_computation | custom fusion | bytes 5244928 | tf_op jit(solution)/shard_map/jit(_take)/gather | solution.py:110
  340.4 22.7 %all-gather.5.cloned.1.call-done = bf16[2560,320]{1,0:T(8,128)(2,1)} async-done(((bf16[320,320]{1,0:T(8,128)(2,1)}), bf16[2560,320]{1,0:T(8,128)(2,1)}) %all-gather.5.cloned.1.call-update) | async-done | bytes 1638416 | tf_op jit(solution)/shard_map/all_gather | solution.py:72
  363.2 3.4 fusion.19
  (26 shorter events, 0.4 us)
Async XLA Ops:
  7.2 187.4 %all-gather.3.cloned.1.call-start = ((), (), s32[]{:S(2)}) async-start(), calls=%async_computation.5 | async-start | bytes 13107200 | tf_op jit(solution)/shard_map/all_gather | solution.py:62
  9.1 64.3 %copy-start.3 = (s32[128]{0:T(128)S(1)}, s32[128]{0:T(128)}, u32[]{:S(2)}) copy-start(s32[128]{0:T(128)} %param.10) | copy-start | bytes 1540
  9.1 71.6 %copy-start = (bf16[128,5120]{1,0:T(8,128)(2,1)S(1)}, bf16[128,5120]{1,0:T(8,128)(2,1)}, u32[]{:S(2)}) copy-start(bf16[128,5120]{1,0:T(8,128)(2,1)} %param.8) | copy-start | bytes 3932164
  74.1 13.3 %all-to-all-start.1 = ((s32[16,1,128]{2,1,0:T(1,128)}), s32[16,1,128]{2,1,0:T(1,128)S(1)}, u32[]{:S(2)}, u32[]{:S(2)}) async-start(s32[16,1,128]{2,1,0:T(1,128)} %broadcast_in_dim.77), calls=%async_computation.1 | async-start | bytes 16384 | tf_op jit(solution)/shard_map/all_to_all | solution.py:55
  87.4 37.0 %all-to-all-start = ((bf16[128,16,320]{0,2,1:T(8,128)(2,1)}), bf16[128,16,320]{0,2,1:T(8,128)(2,1)}, u32[]{:S(2)}, u32[]{:S(2)}) async-start(bf16[128,16,320]{0,2,1:T(8,128)(2,1)} %bitcast.4), calls=%async_computation | async-start | bytes 2621440 | tf_op jit(solution)/shard_map/all_to_all | solution.py:79
  91.8 175.1 %reduce-scatter.7.cloned.1.call-start = ((), (), s32[]{:S(2)}) async-start(), calls=%async_computation.7 | async-start | bytes 3686400
  98.2 3.9 %copy-start.2 = (s32[1,2048]{1,0:T(1,128)S(1)}, s32[1,2048]{1,0:T(1,128)}, u32[]{:S(2)}) copy-start(s32[1,2048]{1,0:T(1,128)} %param.11) | copy-start | bytes 24580
  224.7 87.4 %reduce-scatter.9.cloned.1.call-start = ((), (), s32[]{:S(2)}) async-start(), calls=%async_computation.8 | async-start | bytes 512000
  266.9 96.2 %all-gather.5.cloned.1.call-start = ((), (), s32[]{:S(2)}) async-start(), calls=%async_computation.6 | async-start | bytes 2211840 | tf_op jit(solution)/shard_map/all_gather | solution.py:72
  313.3 27.1 %copy-start.1 = (bf16[80,320]{1,0:T(8,128)(2,1)}, bf16[80,320]{1,0:T(8,128)(2,1)S(1)}, u32[]{:S(2)}) copy-start(bf16[80,320]{1,0:T(8,128)(2,1)S(1)} %copy.37) | copy-start | bytes 153604
Sparse Core Ops, SparseCore 0:
  73.6 120.9 all-gather.2
  224.8 42.0 reduce-scatter.6
  270.0 42.0 reduce-scatter.8
  329.9 33.1 all-gather.4

commit v6 on v2

--- a/solution.py
+++ b/solution.py
@@ -4,6 +4,7 @@
 import jax.numpy as jnp
 import numpy as np
 from jax import lax
+from jax.experimental.layout import Layout, with_layout_constraint
 from jax.sharding import Mesh
 from jax.sharding import PartitionSpec as P
 
@@ -94,6 +95,7 @@
         fisher = fisher / MICRO
         product = fisher * theta_rows.astype(jnp.float32)
         both = jnp.concatenate([product.astype(jnp.bfloat16), fisher.astype(jnp.bfloat16)], axis=1)
+        both = with_layout_constraint(both, Layout(major_to_minor=(0, 1)))
         summed = scatter_sites(both).astype(jnp.float32)
         numerator, denominator = summed[:, :cols], summed[:, cols:]
         owned = (numerator / (denominator + epsilon)).astype(jnp.bfloat16)

time: 373 us -> 374 us (level)
  local copies, waits for them, and re-layouts: 29.4 us -> 21.2 us
  waiting for transfers between devices: 211 us -> 218 us
    unnamed x7 -> x5, waiting for transfers between devices: 89.6 us -> 0.08 us
    reduce_scatter x0 -> x2, waiting for transfers between devices: none -> 89.4 us  [scatter_sites(): x = lax.psum_scatter(x, stage, scatter_dimension=0, tiled=True)]
    all_gather x2, waiting for transfers between devices: 99.7 us -> 106 us  [gather_events(): x = lax.all_gather(x, name, axis=0, tiled=True)]
    unnamed x15 -> x12, local copies, waits for them, and re-layouts: 11.1 us -> 6.51 us
  transfers between devices with their start and end apart: 6 -> 6, of which waited for: 5 -> 5; matrix products, arithmetic and copies ran while one was open for 9% -> 7% of each run, Pallas kernels for 0% -> 0%
where the time goes in v6:
time: 374 us; the launch traced here: 373 us
  waiting for transfers between devices  218 us (58%)
  blocking collectives  70.8 us (19%)
  matrix products  23.5 us (6%)
  local copies, waits for them, and re-layouts  21.2 us (6%)
  other arithmetic  19.6 us (5%)
  between operations  14 us (4%)
  starting transfers between devices  6.06 us (2%)
    all_gather x2, waiting for transfers between devices, gather_events(): x = lax.all_gather(x, name, axis=0, tiled=True)  106 us
    reduce_scatter x2, waiting for transfers between devices, scatter_sites(): x = lax.psum_scatter(x, stage, scatter_dimension=0, tiled=True)  89.4 us
    all_gather x1, blocking collectives, on_device(): site_ids = lax.all_gather(token_ids, shard_names, axis=0, tiled=True)  54.2 us
    all_gather x1, waiting for transfers between devices, gather_sites(): x = lax.all_gather(x, stage, axis=0, tiled=True)  22.7 us
    dot_general x1, matrix products, on_device(): lax.dot_general(site_acts, masked, (((0,), (0,)), ((), ())), preferred_el...  20 us
    all_gather x1, blocking collectives, gather_sites(): x = lax.all_gather(x, stage, axis=0, tiled=True)  16.7 us
    gather x1, local copies, waits for them, and re-layouts, on_device(): probe = jnp.take(site_acts, ordering[:micro_rows], axis=0)  10.5 us
    convert_element_type x1, other arithmetic, on_device(): product.astype(jnp.bfloat16)  8.25 us
  transfers between devices with their start and end apart: 6, of which 5 were waited for; matrix products, arithmetic and copies ran while one was open for 7% of the time, Pallas kernels for 0%

profile of v6, /device:TPU:1, one launch (start us, length us, event | category | flops | bytes accessed | tf_op | source)
XLA Modules:
  0.0 373.4 jit_solution(15080771764118772849)
XLA Ops:
  7.2 0.0 all-gather.5.cloned.1.call-start
  7.2 1.4 copy.28
  8.6 0.0 copy-start
  8.7 1.1 copy.30
  9.8 0.0 all-gather.5.cloned.1.call-update
  9.8 0.0 all-gather.7.cloned.1.call-start
  9.8 69.1 %all-gather.5.cloned.1.call-done = bf16[512,2560]{1,0:T(8,128)(2,1)} async-done(((bf16[128,2560]{1,0:T(8,128)(2,1)}), bf16[512,2560]{1,0:T(8,128)(2,1)}) %all-gather.5.cloned.1.call-update) | async-done | bytes 2621456 | tf_op jit(solution)/shard_map/all_gather | solution.py:55
  78.9 0.0 all-gather.7.cloned.1.call-update
  78.9 0.0 copy-done
  79.0 0.0 copy-start.3
  79.0 1.5 copy.26
  80.4 5.9 %all-to-all-start = ((bf16[128,16,320]{0,2,1:T(8,128)(2,1)}), bf16[128,16,320]{0,2,1:T(8,128)(2,1)S(1)}, u32[]{:S(2)}, u32[]{:S(2)}) async-start(bf16[128,16,320]{0,2,1:T(8,128)(2,1)} %bitcast.3), calls=%async_computation | async-start | bytes 2621440 | tf_op jit(solution)/shard_map/all_to_all | solution.py:72
  86.3 0.0 reduce-scatter.3.cloned.1.call-start
  86.3 0.0 copy-done.3
  86.3 54.2 %all-gather = s32[16,1,128]{2,1,0:T(1,128)S(1)} all-gather(s32[1,1,128]{2,1,0:T(1,128)S(1)} %bitcast.52), channel_id=1, replica_groups=mesh['zh'=4,'y'=4,'c'=2,'x'=4,'zl'=4] {'x','zl'}, dimensions={0}, use_global_device_ids=true | all-gather | bytes 8704 | tf_op jit(solution)/shard_map/all_gather | solution.py:70
  140.5 0.5 broadcast.96
  141.0 0.7 reduce.3
  141.7 2.7 while.10
  141.7 0.6 convert_reduce_fusion.2
  142.4 0.6 convert_reduce_fusion.2
  143.1 0.6 convert_reduce_fusion.2
  143.7 0.6 convert_reduce_fusion.2
  144.4 3.6 copy.32
  148.1 0.4 convert_bitcast_fusion
  148.5 0.0 copy-start.2
  148.5 2.3 copy.33
  150.8 1.7 select_reduce_fusion
  152.5 0.0 all-to-all-done
  152.6 0.4 broadcast_select_fusion.3
  152.9 1.9 broadcast_select_fusion.2
  154.8 36.8 %all-gather.7.cloned.1.call-done = bf16[2048,2560]{1,0:T(8,128)(2,1)} async-done(((bf16[512,2560]{1,0:T(8,128)(2,1)}), bf16[2048,2560]{1,0:T(8,128)(2,1)}) %all-gather.7.cloned.1.call-update) | async-done | bytes 10485776 | tf_op jit(solution)/shard_map/all_gather | solution.py:55
  191.6 20.0 %convolution_bitcast_fusion = f32[2560,1280]{1,0:T(8,128)} fusion(bf16[2048,2560]{1,0:T(8,128)(2,1)} %all-gather.7.cloned.1.call-done, bf16[2048,320]{0,1:T(8,128)(2,1)} %get-tuple-element.39, bf16[2048,320]{0,1:T(8,128)(2,1)} %get-tuple-element.38, bf16[2048,320]{0,1:T(8,128)(2,1)S(1)} %get-tuple-element.37, bf16[2048,320]{0,1:T(8,128)(2,1)S(1)} %get-tuple-element.35), kind=kOutput, calls=%fused_computation.5 | convolution fusion | flops 13442744320 | bytes 28835840 | tf_op jit(solution)/shard_map/dot_general | solution.py:87
  211.6 8.2 %fusion.11 = (bf16[2560,320]{1,0:T(8,128)(2,1)S(1)}, bf16[2560,320]{1,0:T(8,128)(2,1)S(1)}) fusion(f32[4,2,4,80,320]{4,3,2,1,0:T(8,128)} %copy.33, f32[2560,1280]{1,0:T(8,128)} %convolution_bitcast_fusion), kind=kLoop, calls=%fused_computation.23 | loop fusion | flops 9011200 | bytes 19660800 | tf_op jit(solution)/shard_map/convert_element_type | solution.py:97
  219.9 2.9 pad_maximum_fusion
  222.8 0.0 reduce-scatter.3.cloned.1.call-update
  222.8 0.0 reduce-scatter.5.cloned.1.call-start
  222.9 44.8 %reduce-scatter.3.cloned.1.call-done = bf16[320,640]{1,0:T(8,128)(2,1)} async-done(((bf16[2560,640]{1,0:T(8,128)(2,1)}), bf16[320,640]{1,0:T(8,128)(2,1)}) %reduce-scatter.3.cloned.1.call-update) | async-done | bytes 409616 | tf_op jit(solution)/shard_map/reduce_scatter | solution.py:60
  267.6 0.0 reduce-scatter.5.cloned.1.call-update
  267.7 0.0 all-gather.9.cloned.1.call-start
  267.7 44.7 %reduce-scatter.5.cloned.1.call-done = bf16[80,640]{1,0:T(8,128)(2,1)} async-done(((bf16[320,640]{1,0:T(8,128)(2,1)}), bf16[80,640]{1,0:T(8,128)(2,1)}) %reduce-scatter.5.cloned.1.call-update) | async-done | bytes 102416 | tf_op jit(solution)/shard_map/reduce_scatter | solution.py:60
  312.4 0.9 convert_element_type.61
  313.3 0.1 fusion.24
  313.4 0.0 copy-start.1
  313.4 16.7 %all_gather.18 = bf16[320,320]{1,0:T(8,128)(2,1)} all-gather(bf16[80,320]{1,0:T(8,128)(2,1)S(1)} %fusion.24), channel_id=1, replica_groups=mesh['zh'=4,'y'=4,'c'=2,'x'=4,'zl'=4] {'zh'}, dimensions={0}, use_global_device_ids=true | all-gather | bytes 256000 | tf_op jit(solution)/shard_map/all_gather | solution.py:65
  330.1 0.0 all-gather.9.cloned.1.call-update
  330.2 10.5 %gather_fusion = bf16[512,2560]{1,0:T(8,128)(2,1)S(1)} fusion(bf16[2048,2560]{1,0:T(8,128)(2,1)} %all-gather.7.cloned.1.call-done, s32[1024]{0:T(1024)S(1)} %pad_clamp_fusion), kind=kCustom, calls=%fused_computation | custom fusion | bytes 5244928 | tf_op jit(solution)/shard_map/jit(_take)/gather | solution.py:104
  340.7 22.7 %all-gather.9.cloned.1.call-done = bf16[2560,320]{1,0:T(8,128)(2,1)} async-done(((bf16[320,320]{1,0:T(8,128)(2,1)}), bf16[2560,320]{1,0:T(8,128)(2,1)}) %all-gather.9.cloned.1.call-update) | async-done | bytes 1638416 | tf_op jit(solution)/shard_map/all_gather | solution.py:65
  363.4 3.4 fusion.20
  (21 shorter events, 0.3 us)
Async XLA Ops:
  7.2 71.8 %all-gather.5.cloned.1.call-start = ((), (), s32[]{:S(2)}) async-start(), calls=%async_computation.3 | async-start | bytes 3276800 | tf_op jit(solution)/shard_map/all_gather | solution.py:55
  8.6 70.3 %copy-start = (bf16[128,5120]{1,0:T(8,128)(2,1)S(1)}, bf16[128,5120]{1,0:T(8,128)(2,1)}, u32[]{:S(2)}) copy-start(bf16[128,5120]{1,0:T(8,128)(2,1)} %param.8) | copy-start | bytes 3932164
  9.8 181.8 %all-gather.7.cloned.1.call-start = ((), (), s32[]{:S(2)}) async-start(), calls=%async_computation.4 | async-start | bytes 13107200 | tf_op jit(solution)/shard_map/all_gather | solution.py:55
  79.0 7.4 %copy-start.3 = (s32[128]{0:T(128)S(1)}, s32[128]{0:T(128)}, u32[]{:S(2)}) copy-start(s32[128]{0:T(128)} %param.10) | copy-start | bytes 1540
  80.4 72.1 %all-to-all-start = ((bf16[128,16,320]{0,2,1:T(8,128)(2,1)}), bf16[128,16,320]{0,2,1:T(8,128)(2,1)S(1)}, u32[]{:S(2)}, u32[]{:S(2)}) async-start(bf16[128,16,320]{0,2,1:T(8,128)(2,1)} %bitcast.3), calls=%async_computation | async-start | bytes 2621440 | tf_op jit(solution)/shard_map/all_to_all | solution.py:72
  86.3 181.3 %reduce-scatter.3.cloned.1.call-start = ((), (), s32[]{:S(2)}) async-start(), calls=%async_computation.5 | async-start | bytes 3686400 | tf_op jit(solution)/shard_map/reduce_scatter | solution.py:60
  148.5 2.3 copy-start.2
  222.8 89.6 %reduce-scatter.5.cloned.1.call-start = ((), (), s32[]{:S(2)}) async-start(), calls=%async_computation.6 | async-start | bytes 512000 | tf_op jit(solution)/shard_map/reduce_scatter | solution.py:60
  267.7 95.7 %all-gather.9.cloned.1.call-start = ((), (), s32[]{:S(2)}) async-start(), calls=%async_computation.7 | async-start | bytes 2211840 | tf_op jit(solution)/shard_map/all_gather | solution.py:65
  313.4 27.3 %copy-start.1 = (bf16[80,320]{1,0:T(8,128)(2,1)}, bf16[80,320]{1,0:T(8,128)(2,1)S(1)}, u32[]{:S(2)}) copy-start(bf16[80,320]{1,0:T(8,128)(2,1)S(1)} %fusion.24) | copy-start | bytes 153604
Sparse Core Ops, SparseCore 0:
  10.1 68.7 all-gather.4
  81.0 110.5 all-gather.6
  222.9 44.6 reduce-scatter.2
  270.6 41.7 reduce-scatter.4
  330.2 33.1 all-gather.8

commit v7 on v2

--- a/solution.py
+++ b/solution.py
@@ -60,7 +60,11 @@
         return x
 
     def gather_sites(x):
-        for stage in reversed(scatter_stages):
+        stages = tuple(reversed(scatter_stages))
+        group = math.prod(size for name, size in site_axes if name in stages[0])
+        copies = jnp.broadcast_to(x[None], (group,) + x.shape)
+        x = lax.all_to_all(copies, stages[0], 0, 0, tiled=True).reshape((group * x.shape[0],) + x.shape[1:])
+        for stage in stages[1:]:
             x = lax.all_gather(x, stage, axis=0, tiled=True)
         return x
 

time: 373 us -> 374 us (level)
    all_to_all x0 -> x1, blocking collectives: none -> 20.7 us  [gather_sites(): lax.all_to_all(copies, stages[0], 0, 0, tiled=True)]
    all_gather x1 -> x0, blocking collectives: 17.1 us -> none  [gather_sites(): x = lax.all_gather(x, stage, axis=0, tiled=True)]
where the time goes in v7:
time: 374 us; the launch traced here: 373 us
  waiting for transfers between devices  209 us (56%)
  blocking collectives  74.8 us (20%)
  local copies, waits for them, and re-layouts  29.4 us (8%)
  matrix products  24.2 us (6%)
  other arithmetic  15.9 us (4%)
  between operations  14 us (4%)
  starting transfers between devices  6.28 us (2%)
    all_gather x2, waiting for transfers between devices, gather_events(): x = lax.all_gather(x, name, axis=0, tiled=True)  99.7 us
    unnamed x7, waiting for transfers between devices  89.4 us
    all_gather x1, blocking collectives, on_device(): site_ids = lax.all_gather(token_ids, shard_names, axis=0, tiled=True)  54.1 us
    dot_general x1, matrix products, on_device(): lax.dot_general(site_acts, masked, (((0,), (0,)), ((), ())), preferred_el...  20.7 us
    all_to_all x1, blocking collectives, gather_sites(): lax.all_to_all(copies, stages[0], 0, 0, tiled=True)  20.7 us
    all_gather x1, waiting for transfers between devices, gather_sites(): x = lax.all_gather(x, stage, axis=0, tiled=True)  19.6 us
    unnamed x15, local copies, waits for them, and re-layouts  11.1 us
    gather x1, local copies, waits for them, and re-layouts, on_device(): probe = jnp.take(site_acts, ordering[:micro_rows], axis=0)  10.5 us
  transfers between devices with their start and end apart: 6, of which 5 were waited for; matrix products, arithmetic and copies ran while one was open for 9% of the time, Pallas kernels for 0%

profile of v7, /device:TPU:1, one launch (start us, length us, event | category | flops | bytes accessed | tf_op | source)
XLA Modules:
  0.0 373.5 jit_solution(13591102099890963531)
XLA Ops:
  7.2 0.0 all-gather.5.cloned.1.call-start
  7.2 1.4 copy.33
  8.6 0.0 copy-start
  8.7 1.1 copy.35
  9.8 0.0 all-gather.5.cloned.1.call-update
  9.8 0.0 all-gather.7.cloned.1.call-start
  9.9 69.1 %all-gather.5.cloned.1.call-done = bf16[512,2560]{1,0:T(8,128)(2,1)} async-done(((bf16[128,2560]{1,0:T(8,128)(2,1)}), bf16[512,2560]{1,0:T(8,128)(2,1)}) %all-gather.5.cloned.1.call-update) | async-done | bytes 2621456 | tf_op jit(solution)/shard_map/all_gather | solution.py:54
  78.9 0.0 all-gather.7.cloned.1.call-update
  78.9 0.0 copy-done
  79.0 0.0 copy-start.3
  79.0 1.5 copy.31
  80.5 5.9 %all-to-all-start = ((bf16[128,16,320]{0,2,1:T(8,128)(2,1)}), bf16[128,16,320]{0,2,1:T(8,128)(2,1)}, u32[]{:S(2)}, u32[]{:S(2)}) async-start(bf16[128,16,320]{0,2,1:T(8,128)(2,1)} %bitcast.3), calls=%async_computation | async-start | bytes 2621440 | tf_op jit(solution)/shard_map/all_to_all | solution.py:75
  86.4 0.0 reduce-scatter.7.cloned.1.call-start
  86.5 54.1 %all-gather = s32[16,1,128]{2,1,0:T(1,128)S(1)} all-gather(s32[1,1,128]{2,1,0:T(1,128)S(1)} %bitcast.54), channel_id=1, replica_groups=mesh['zh'=4,'y'=4,'c'=2,'x'=4,'zl'=4] {'x','zl'}, dimensions={0}, use_global_device_ids=true | all-gather | bytes 8704 | tf_op jit(solution)/shard_map/all_gather | solution.py:73
  140.6 0.5 broadcast.97
  141.1 0.7 reduce.3
  141.8 2.7 while.10
  141.8 0.6 convert_reduce_fusion.2
  142.5 0.6 convert_reduce_fusion.2
  143.1 0.6 convert_reduce_fusion.2
  143.8 0.6 convert_reduce_fusion.2
  144.5 3.6 copy.36
  148.1 0.4 convert_bitcast_fusion
  148.5 2.2 copy.37
  150.7 3.7 copy.38
  154.4 1.7 select_reduce_fusion
  156.2 0.0 all-to-all-done
  156.2 2.8 broadcast_select_fusion.3
  158.9 2.0 broadcast_select_fusion.2
  161.0 30.7 %all-gather.7.cloned.1.call-done = bf16[2048,2560]{1,0:T(8,128)(2,1)} async-done(((bf16[512,2560]{1,0:T(8,128)(2,1)}), bf16[2048,2560]{1,0:T(8,128)(2,1)}) %all-gather.7.cloned.1.call-update) | async-done | bytes 10485776 | tf_op jit(solution)/shard_map/all_gather | solution.py:54
  191.6 20.7 %convolution_bitcast_fusion = f32[2560,1280]{0,1:T(8,128)} fusion(bf16[2048,2560]{1,0:T(8,128)(2,1)} %all-gather.7.cloned.1.call-done, bf16[2048,320]{0,1:T(8,128)(2,1)} %get-tuple-element.47, bf16[2048,320]{0,1:T(8,128)(2,1)} %get-tuple-element.46, bf16[2048,320]{0,1:T(8,128)(2,1)} %get-tuple-element.45, bf16[2048,320]{0,1:T(8,128)(2,1)} %get-tuple-element.43), kind=kOutput, calls=%fused_computation.5 | convolution fusion | flops 13442744320 | bytes 28835840 | tf_op jit(solution)/shard_map/dot_general | solution.py:90
  212.4 5.7 %multiply_convert_fusion = (bf16[2560,320]{0,1:T(8,128)(2,1)S(1)}, bf16[2560,320]{0,1:T(8,128)(2,1)S(1)}) fusion(f32[2560,320]{0,1:T(8,128)S(1)} %copy.38, f32[2560,1280]{0,1:T(8,128)} %convolution_bitcast_fusion), kind=kLoop, calls=%fused_computation.23 | loop fusion | flops 9011200 | bytes 19660800 | tf_op jit(solution)/shard_map/convert_element_type | solution.py:100
  218.1 0.2 pad_maximum_fusion
  218.3 3.4 copy.41
  221.7 0.0 reduce-scatter.7.cloned.1.call-update
  221.7 0.0 reduce-scatter.9.cloned.1.call-start
  221.8 44.8 %reduce-scatter.7.cloned.1.call-done = bf16[320,640]{1,0:T(8,128)(2,1)} async-done(((bf16[2560,640]{1,0:T(8,128)(2,1)}), bf16[320,640]{1,0:T(8,128)(2,1)}) %reduce-scatter.7.cloned.1.call-update) | async-done | bytes 409616
  266.5 0.0 reduce-scatter.9.cloned.1.call-update
  266.5 0.2 all-gather.9.cloned.1.call-start
  266.8 44.6 %reduce-scatter.9.cloned.1.call-done = bf16[80,640]{1,0:T(8,128)(2,1)} async-done(((bf16[320,640]{1,0:T(8,128)(2,1)}), bf16[80,640]{1,0:T(8,128)(2,1)}) %reduce-scatter.9.cloned.1.call-update) | async-done | bytes 102416
  311.3 1.1 copy.44
  312.5 0.1 copy.40
  312.6 0.0 copy-start.1
  312.6 20.7 %all_to_all.18 = bf16[4,80,320]{2,1,0:T(8,128)(2,1)} all-to-all(bf16[4,80,320]{2,1,0:T(8,128)(2,1)S(1)} %broadcast_in_dim.76), channel_id=1, replica_groups=mesh['zh'=4,'y'=4,'c'=2,'x'=4,'zl'=4] {'zh'}, dimensions={0} | all-to-all | bytes 409600 | tf_op jit(solution)/shard_map/all_to_all | solution.py:66
  333.3 0.0 all-gather.9.cloned.1.call-update
  333.4 10.5 %gather_fusion = bf16[512,2560]{1,0:T(8,128)(2,1)S(1)} fusion(bf16[2048,2560]{1,0:T(8,128)(2,1)} %all-gather.7.cloned.1.call-done, s32[1024]{0:T(1024)S(1)} %pad_clamp_fusion), kind=kCustom, calls=%fused_computation | custom fusion | bytes 5244928 | tf_op jit(solution)/shard_map/jit(_take)/gather | solution.py:106
  343.9 19.6 %all-gather.9.cloned.1.call-done = bf16[2560,320]{1,0:T(8,128)(2,1)} async-done(((bf16[320,320]{1,0:T(8,128)(2,1)}), bf16[2560,320]{1,0:T(8,128)(2,1)}) %all-gather.9.cloned.1.call-update) | async-done | bytes 1638416 | tf_op jit(solution)/shard_map/all_gather | solution.py:68
  363.5 3.4 fusion.19
  (26 shorter events, 0.4 us)
Async XLA Ops:
  7.2 71.8 %all-gather.5.cloned.1.call-start = ((), (), s32[]{:S(2)}) async-start(), calls=%async_computation.4 | async-start | bytes 3276800 | tf_op jit(solution)/shard_map/all_gather | solution.py:54
  8.6 70.3 %copy-start = (bf16[128,5120]{1,0:T(8,128)(2,1)S(1)}, bf16[128,5120]{1,0:T(8,128)(2,1)}, u32[]{:S(2)}) copy-start(bf16[128,5120]{1,0:T(8,128)(2,1)} %param.8) | copy-start | bytes 3932164
  9.8 181.8 %all-gather.7.cloned.1.call-start = ((), (), s32[]{:S(2)}) async-start(), calls=%async_computation.5 | async-start | bytes 13107200 | tf_op jit(solution)/shard_map/all_gather | solution.py:54
  79.0 7.5 %copy-start.3 = (s32[128]{0:T(128)S(1)}, s32[128]{0:T(128)}, u32[]{:S(2)}) copy-start(s32[128]{0:T(128)} %param.10) | copy-start | bytes 1540
  80.5 75.7 %all-to-all-start = ((bf16[128,16,320]{0,2,1:T(8,128)(2,1)}), bf16[128,16,320]{0,2,1:T(8,128)(2,1)}, u32[]{:S(2)}, u32[]{:S(2)}) async-start(bf16[128,16,320]{0,2,1:T(8,128)(2,1)} %bitcast.3), calls=%async_computation | async-start | bytes 2621440 | tf_op jit(solution)/shard_map/all_to_all | solution.py:75
  86.4 180.1 %reduce-scatter.7.cloned.1.call-start = ((), (), s32[]{:S(2)}) async-start(), calls=%async_computation.7 | async-start | bytes 3686400
  150.7 3.7 copy-start.2
  221.7 89.6 %reduce-scatter.9.cloned.1.call-start = ((), (), s32[]{:S(2)}) async-start(), calls=%async_computation.8 | async-start | bytes 512000
  266.5 97.0 %all-gather.9.cloned.1.call-start = ((), (), s32[]{:S(2)}) async-start(), calls=%async_computation.6 | async-start | bytes 2211840 | tf_op jit(solution)/shard_map/all_gather | solution.py:68
  312.6 31.3 %copy-start.1 = (bf16[80,320]{1,0:T(8,128)(2,1)}, bf16[80,320]{1,0:T(8,128)(2,1)S(1)}, u32[]{:S(2)}) copy-start(bf16[80,320]{1,0:T(8,128)(2,1)S(1)} %copy.40) | copy-start | bytes 153604
Sparse Core Ops, SparseCore 0:
  10.1 68.7 all-gather.4
  81.0 110.5 all-gather.6
  221.8 44.6 reduce-scatter.6
  269.4 41.8 reduce-scatter.8
  333.4 30.0 all-gather.8

commit v8 on v2

--- a/solution.py
+++ b/solution.py
@@ -66,7 +66,9 @@
 
     def on_device(activations, out_grads, theta, token_ids, assignment):
         head_cols = HEADS * HEAD_DIM
-        site_ids = lax.all_gather(token_ids, shard_names, axis=0, tiled=True)
+        group = math.prod(size for _, size in shard_axes)
+        id_copies = jnp.broadcast_to(token_ids[None], (group,) + token_ids.shape)
+        site_ids = lax.all_to_all(id_copies, shard_names, 0, 0, tiled=True).reshape(-1)
         site_acts = gather_events(to_position_order(activations, 1))
         grad_cols = lax.all_to_all(out_grads, shard_names, split_axis=1, concat_axis=0, tiled=True)
         theta_rows = to_position_order(theta[0], 0)

time: 373 us -> 377 us (1.011)
  blocking collectives: 71.2 us -> 16.4 us
  waiting for transfers between devices: 211 us -> 265 us
  starting transfers between devices: 6.1 us -> 10.4 us
    all_gather x1 -> x0, blocking collectives: 54.1 us -> none  [on_device(): site_ids = lax.all_gather(token_ids, shard_names, axis=0, tiled=True)]
    all_gather x2, waiting for transfers between devices: 99.7 us -> 134 us  [gather_events(): x = lax.all_gather(x, name, axis=0, tiled=True)]
    all_to_all x1, waiting for transfers between devices: 0.01 us -> 16.7 us  [on_device(): lax.all_to_all(out_grads, shard_names, split_axis=1, concat_axis=0, tiled...]
    all_to_all x0 -> x1, starting transfers between devices: none -> 5.86 us  [on_device(): lax.all_to_all(id_copies, shard_names, 0, 0, tiled=True).reshape(-1)]
    all_to_all x0 -> x1, waiting for transfers between devices: none -> 5.11 us  [on_device(): lax.all_to_all(id_copies, shard_names, 0, 0, tiled=True).reshape(-1)]
  transfers between devices with their start and end apart: 6 -> 7, of which waited for: 5 -> 7; matrix products, arithmetic and copies ran while one was open for 9% -> 9% of each run, Pallas kernels for 0% -> 0%
where the time goes in v8:
time: 377 us; the launch traced here: 376 us
  waiting for transfers between devices  265 us (70%)
  local copies, waits for them, and re-layouts  30.3 us (8%)
  matrix products  24.2 us (6%)
  blocking collectives  16.4 us (4%)
  other arithmetic  16 us (4%)
  between operations  14 us (4%)
  starting transfers between devices  10.4 us (3%)
    all_gather x2, waiting for transfers between devices, gather_events(): x = lax.all_gather(x, name, axis=0, tiled=True)  134 us
    unnamed x7, waiting for transfers between devices  85.9 us
    all_gather x1, waiting for transfers between devices, gather_sites(): x = lax.all_gather(x, stage, axis=0, tiled=True)  22.8 us
    dot_general x1, matrix products, on_device(): lax.dot_general(site_acts, masked, (((0,), (0,)), ((), ())), preferred_el...  20.7 us
    all_to_all x1, waiting for transfers between devices, on_device(): lax.all_to_all(out_grads, shard_names, split_axis=1, concat_axis=0, tiled...  16.7 us
    all_gather x1, blocking collectives, gather_sites(): x = lax.all_gather(x, stage, axis=0, tiled=True)  16.4 us
    unnamed x15, local copies, waits for them, and re-layouts  11.2 us
    gather x1, local copies, waits for them, and re-layouts, on_device(): probe = jnp.take(site_acts, ordering[:micro_rows], axis=0)  10.5 us
  transfers between devices with their start and end apart: 7, of which 7 were waited for; matrix products, arithmetic and copies ran while one was open for 9% of the time, Pallas kernels for 0%

profile of v8, /device:TPU:1, one launch (start us, length us, event | category | flops | bytes accessed | tf_op | source)
XLA Modules:
  0.0 376.4 jit_solution(12061397331673780838)
XLA Ops:
  7.2 0.0 all-gather.4.cloned.1.call-start
  7.2 1.4 copy.31
  8.6 0.0 copy-start.3
  8.7 1.1 copy.33
  9.8 0.0 all-gather.4.cloned.1.call-update
  9.8 0.0 all-gather.6.cloned.1.call-start
  9.9 69.0 %all-gather.4.cloned.1.call-done = bf16[512,2560]{1,0:T(8,128)(2,1)} async-done(((bf16[128,2560]{1,0:T(8,128)(2,1)}), bf16[512,2560]{1,0:T(8,128)(2,1)}) %all-gather.4.cloned.1.call-update) | async-done | bytes 2621456 | tf_op jit(solution)/shard_map/all_gather | solution.py:54
  78.9 0.0 all-gather.6.cloned.1.call-update
  79.0 0.6 broadcast_in_dim.70
  79.6 5.9 %all-to-all-start.1 = ((s32[16,1,128]{2,1,0:T(1,128)}), s32[16,1,128]{2,1,0:T(1,128)S(1)}, u32[]{:S(2)}, u32[]{:S(2)}) async-start(s32[16,1,128]{2,1,0:T(1,128)} %broadcast_in_dim.70), calls=%async_computation.1 | async-start | bytes 16384 | tf_op jit(solution)/shard_map/all_to_all | solution.py:71
  85.4 1.5 copy.29
  87.0 5.1 %all-to-all-done.1 = s32[16,1,128]{2,1,0:T(1,128)S(1)} async-done(((s32[16,1,128]{2,1,0:T(1,128)}), s32[16,1,128]{2,1,0:T(1,128)S(1)}, u32[]{:S(2)}, u32[]{:S(2)}) %all-to-all-start.1) | async-done | bytes 8224 | tf_op jit(solution)/shard_map/all_to_all | solution.py:71
  92.1 4.4 %all-to-all-start = ((bf16[128,16,320]{0,2,1:T(8,128)(2,1)}), bf16[128,16,320]{0,2,1:T(8,128)(2,1)}, u32[]{:S(2)}, u32[]{:S(2)}) async-start(bf16[128,16,320]{0,2,1:T(8,128)(2,1)} %bitcast.4), calls=%async_computation | async-start | bytes 2621440 | tf_op jit(solution)/shard_map/all_to_all | solution.py:73
  96.5 0.0 reduce-scatter.7.cloned.1.call-start
  96.5 3.7 copy.34
  100.2 0.4 convert_bitcast_fusion
  100.7 2.2 copy.35
  102.8 3.9 %copy.36 = f32[2560,320]{0,1:T(8,128)S(1)} copy(f32[2560,320]{1,0:T(8,128)} %bitcast.43) | data formatting | bytes 6553600 | tf_op jit(solution)/shard_map/convert_element_type | solution.py:97
  106.7 1.7 select_reduce_fusion
  108.5 0.5 broadcast.98
  109.0 0.7 reduce.3
  109.7 2.7 while.10
  109.7 0.6 convert_reduce_fusion.2
  110.4 0.6 convert_reduce_fusion.2
  111.1 0.6 convert_reduce_fusion.2
  111.7 0.6 convert_reduce_fusion.2
  112.4 16.7 %all-to-all-done = bf16[128,16,320]{0,2,1:T(8,128)(2,1)} async-done(((bf16[128,16,320]{0,2,1:T(8,128)(2,1)}), bf16[128,16,320]{0,2,1:T(8,128)(2,1)}, u32[]{:S(2)}, u32[]{:S(2)}) %all-to-all-start) | async-done | bytes 1310752 | tf_op jit(solution)/shard_map/all_to_all | solution.py:73
  129.1 2.8 broadcast_select_fusion.3
  131.9 2.0 broadcast_select_fusion.2
  133.9 65.3 %all-gather.6.cloned.1.call-done = bf16[2048,2560]{1,0:T(8,128)(2,1)} async-done(((bf16[512,2560]{1,0:T(8,128)(2,1)}), bf16[2048,2560]{1,0:T(8,128)(2,1)}) %all-gather.6.cloned.1.call-update) | async-done | bytes 10485776 | tf_op jit(solution)/shard_map/all_gather | solution.py:54
  199.3 20.7 %convolution_bitcast_fusion = f32[2560,1280]{0,1:T(8,128)} fusion(bf16[2048,2560]{1,0:T(8,128)(2,1)} %all-gather.6.cloned.1.call-done, bf16[2048,320]{0,1:T(8,128)(2,1)} %get-tuple-element.47, bf16[2048,320]{0,1:T(8,128)(2,1)} %get-tuple-element.46, bf16[2048,320]{0,1:T(8,128)(2,1)} %get-tuple-element.45, bf16[2048,320]{0,1:T(8,128)(2,1)} %get-tuple-element.43), kind=kOutput, calls=%fused_computation.5 | convolution fusion | flops 13442744320 | bytes 28835840 | tf_op jit(solution)/shard_map/dot_general | solution.py:88
  220.0 5.7 %multiply_convert_fusion = (bf16[2560,320]{0,1:T(8,128)(2,1)S(1)}, bf16[2560,320]{0,1:T(8,128)(2,1)S(1)}) fusion(f32[2560,320]{0,1:T(8,128)S(1)} %copy.36, f32[2560,1280]{0,1:T(8,128)} %convolution_bitcast_fusion), kind=kLoop, calls=%fused_computation.23 | loop fusion | flops 9011200 | bytes 19660800 | tf_op jit(solution)/shard_map/convert_element_type | solution.py:98
  225.7 0.2 pad_maximum_fusion
  225.9 3.4 copy.39
  229.3 0.0 reduce-scatter.7.cloned.1.call-update
  229.3 0.0 reduce-scatter.9.cloned.1.call-start
  229.4 40.9 %reduce-scatter.7.cloned.1.call-done = bf16[320,640]{1,0:T(8,128)(2,1)} async-done(((bf16[2560,640]{1,0:T(8,128)(2,1)}), bf16[320,640]{1,0:T(8,128)(2,1)}) %reduce-scatter.7.cloned.1.call-update) | async-done | bytes 409616
  270.3 0.0 reduce-scatter.9.cloned.1.call-update
  270.4 0.0 all-gather.8.cloned.1.call-start
  270.4 44.9 %reduce-scatter.9.cloned.1.call-done = bf16[80,640]{1,0:T(8,128)(2,1)} async-done(((bf16[320,640]{1,0:T(8,128)(2,1)}), bf16[80,640]{1,0:T(8,128)(2,1)}) %reduce-scatter.9.cloned.1.call-update) | async-done | bytes 102416
  315.3 1.1 copy.42
  316.4 0.1 copy.38
  316.5 0.0 copy-start.1
  316.6 16.4 %all_gather.14 = bf16[320,320]{1,0:T(8,128)(2,1)} all-gather(bf16[80,320]{1,0:T(8,128)(2,1)S(1)} %copy.38), channel_id=1, replica_groups=mesh['zh'=4,'y'=4,'c'=2,'x'=4,'zl'=4] {'zh'}, dimensions={0}, use_global_device_ids=true | all-gather | bytes 256000 | tf_op jit(solution)/shard_map/all_gather | solution.py:64
  332.9 0.0 all-gather.8.cloned.1.call-update
  333.0 10.5 %gather_fusion = bf16[512,2560]{1,0:T(8,128)(2,1)S(1)} fusion(bf16[2048,2560]{1,0:T(8,128)(2,1)} %all-gather.6.cloned.1.call-done, s32[1024]{0:T(1024)S(1)} %pad_clamp_fusion), kind=kCustom, calls=%fused_computation | custom fusion | bytes 5244928 | tf_op jit(solution)/shard_map/jit(_take)/gather | solution.py:104
  343.6 22.8 %all-gather.8.cloned.1.call-done = bf16[2560,320]{1,0:T(8,128)(2,1)} async-done(((bf16[320,320]{1,0:T(8,128)(2,1)}), bf16[2560,320]{1,0:T(8,128)(2,1)}) %all-gather.8.cloned.1.call-update) | async-done | bytes 1638416 | tf_op jit(solution)/shard_map/all_gather | solution.py:64
  366.4 3.4 fusion.19
  (27 shorter events, 0.4 us)
Async XLA Ops:
  7.2 71.8 %all-gather.4.cloned.1.call-start = ((), (), s32[]{:S(2)}) async-start(), calls=%async_computation.4 | async-start | bytes 3276800 | tf_op jit(solution)/shard_map/all_gather | solution.py:54
  8.6 70.3 %copy-start.3 = (s32[128]{0:T(128)S(1)}, s32[128]{0:T(128)}, u32[]{:S(2)}) copy-start(s32[128]{0:T(128)} %param.10) | copy-start | bytes 1540
  8.6 76.8 %copy-start = (bf16[128,5120]{1,0:T(8,128)(2,1)S(1)}, bf16[128,5120]{1,0:T(8,128)(2,1)}, u32[]{:S(2)}) copy-start(bf16[128,5120]{1,0:T(8,128)(2,1)} %param.8) | copy-start | bytes 3932164
  9.8 189.4 %all-gather.6.cloned.1.call-start = ((), (), s32[]{:S(2)}) async-start(), calls=%async_computation.5 | async-start | bytes 13107200 | tf_op jit(solution)/shard_map/all_gather | solution.py:54
  79.6 12.5 %all-to-all-start.1 = ((s32[16,1,128]{2,1,0:T(1,128)}), s32[16,1,128]{2,1,0:T(1,128)S(1)}, u32[]{:S(2)}, u32[]{:S(2)}) async-start(s32[16,1,128]{2,1,0:T(1,128)} %broadcast_in_dim.70), calls=%async_computation.1 | async-start | bytes 16384 | tf_op jit(solution)/shard_map/all_to_all | solution.py:71
  92.1 37.0 %all-to-all-start = ((bf16[128,16,320]{0,2,1:T(8,128)(2,1)}), bf16[128,16,320]{0,2,1:T(8,128)(2,1)}, u32[]{:S(2)}, u32[]{:S(2)}) async-start(bf16[128,16,320]{0,2,1:T(8,128)(2,1)} %bitcast.4), calls=%async_computation | async-start | bytes 2621440 | tf_op jit(solution)/shard_map/all_to_all | solution.py:73
  96.5 173.9 %reduce-scatter.7.cloned.1.call-start = ((), (), s32[]{:S(2)}) async-start(), calls=%async_computation.7 | async-start | bytes 3686400
  102.8 3.9 %copy-start.2 = (s32[1,2048]{1,0:T(1,128)S(1)}, s32[1,2048]{1,0:T(1,128)}, u32[]{:S(2)}) copy-start(s32[1,2048]{1,0:T(1,128)} %param.11) | copy-start | bytes 24580
  229.3 86.0 %reduce-scatter.9.cloned.1.call-start = ((), (), s32[]{:S(2)}) async-start(), calls=%async_computation.8 | async-start | bytes 512000
  270.4 96.0 %all-gather.8.cloned.1.call-start = ((), (), s32[]{:S(2)}) async-start(), calls=%async_computation.6 | async-start | bytes 2211840 | tf_op jit(solution)/shard_map/all_gather | solution.py:64
  316.5 27.0 %copy-start.1 = (bf16[80,320]{1,0:T(8,128)(2,1)}, bf16[80,320]{1,0:T(8,128)(2,1)S(1)}, u32[]{:S(2)}) copy-start(bf16[80,320]{1,0:T(8,128)(2,1)S(1)} %copy.38) | copy-start | bytes 153604
Sparse Core Ops, SparseCore 0:
  10.1 68.7 all-gather.3
  81.0 118.1 all-gather.5
  229.5 40.8 reduce-scatter.6
  273.2 42.0 reduce-scatter.8
  333.1 33.2 all-gather.7
